TPU v7x, 256 devices: a whole 4x4x8 slice. The times are simulated.
256 devices in a mesh: grp: 32 (over y, z_lo, core), tp: 8 (over x, z_hi).
Axes of the slice: x: 4, y: 4, z: 8 (z_hi: 2, z_lo: 4; z = z_hi * 4 + z_lo), core: 2. Of those that a mesh axis runs over, the one named last changes fastest.
Arguments:
- tok_ids: int32 [8192], P('grp'), may hold values from 0 to 16383
- accept: int32 [8192], P('grp'), may hold values 0 or 1
- sub_ids: int32 [8192], P('grp'), may hold values from 0 to 16383
- cache_len: int32 [32], replicated, may hold values from 256 to 3840, as said below
- spill: int32 [32], replicated, may hold values from 0 to 1792, as said below
- embed: bfloat16 [16384, 2048], P('grp', 'tp'), may hold values from -6 to 6
- attn_gain: float32 [2048], replicated, may hold values from 0.25 to 1.75
- w_query: bfloat16 [2048, 2048], P(None, 'tp'), may hold values from -0.125 to 0.125
- w_key: bfloat16 [2048, 512], P(None, 'tp'), as said below
- w_value: bfloat16 [2048, 512], P(None, 'tp'), as said below
- w_out: bfloat16 [2048, 2048], P('tp'), may hold values from -2.5 to 2.5
- mlp_gain: float32 [2048], replicated, may hold values from 0.25 to 1.75
- w_gate: bfloat16 [2048, 5632], P(None, 'tp'), may hold values from -0.125 to 0.125
- w_up: bfloat16 [2048, 5632], P(None, 'tp'), may hold values from -0.125 to 0.125
- w_down: bfloat16 [5632, 2048], P('tp'), may hold values from -0.078125 to 0.078125
- cache_keys: bfloat16 [65536, 512], P('grp', 'tp'), may hold values from -320 to 320, as said below
- cache_values: bfloat16 [65536, 512], P('grp', 'tp'), may hold values from -8 to 8, as said below
Outputs:
- first_out: bfloat16 [8192, 2048], P('grp', 'tp')
- second_out: bfloat16 [8192, 2048], P('grp', 'tp')
Inputs may be any that keep to these rules, and one draw needn't show every extreme that they name: Request g keeps cache_len[g] - spill[g] >= 256 positions in slots from 0 of store g and spill[g] positions in the last slots of store (g xor 1); for every g, cache_len[g] - spill[g] + spill[g xor 1] <= 2048. Of each pair of groups 2k, 2k + 1 at most one has spill above 0. `w_key`: the 2 stored copies of a key-value head are equal. `w_value`: the 2 stored copies of a key-value head are equal. `cache_keys`: the 2 stored copies of a key-value head are equal. `cache_values`: the 2 stored copies of a key-value head are equal.
All inputs are finite; a program needn't handle non-finite values. No bound on the sum of `accept` on one device may be relied on, other than what follows from the above.
Results may differ from a plain program's by a relative error of at most 0.024.
Values may be sent and summed in bfloat16 or wider, within the bound.
No kernel may reach another device: no remote copies, remote signals or barrier semaphores. Data moves between devices by JAX's collectives and lax.ppermute only.
A program may use at most 128 MiB of HBM per device.

v0:
```python
import jax
import jax.numpy as jnp
from jax import lax
from jax.sharding import PartitionSpec as P

HD = 64


EPSILON = 1e-05
SENTINEL = -1e30


def swapped(array, axis, bit):
    return lax.ppermute(array, axis, [(i, i ^ 1 << bit) for i in range(lax.axis_size(axis))])


def rms_normed(values, gain):
    square = jnp.mean(values * values, axis=-1, keepdims=True)
    return (values * lax.rsqrt(square + EPSILON) * gain).astype(jnp.bfloat16)


def rotate(vectors, positions):
    half = vectors.shape[-1] // 2
    exponent = jnp.arange(half, dtype=jnp.float32) * (-2.0 / vectors.shape[-1])
    freqs = jnp.power(jnp.float32(10000.0), exponent)
    angles = positions.astype(jnp.float32)[:, None] * freqs[None, :]
    cosine = jnp.cos(angles)[:, None, :]
    sine = jnp.sin(angles)[:, None, :]
    first = vectors[..., :half]
    second = vectors[..., half:]
    return jnp.concatenate(
        [first * cosine - second * sine, second * cosine + first * sine], axis=-1
    )


def partial_attention(query, keys, values, valid):
    scores = jnp.einsum("bcgd,kcd->bcgk", query, keys, preferred_element_type=jnp.float32) * 0.125
    scores = jnp.where(valid, scores, SENTINEL)
    top = jnp.max(scores, axis=-1)
    weights = jnp.where(valid, jnp.exp(scores - top[..., None]), 0.0)
    total = jnp.sum(weights, axis=-1)
    weighted = jnp.einsum(
        "bcgk,kcd->bcgd", weights.astype(jnp.bfloat16), values, preferred_element_type=jnp.float32
    )
    return (weighted, top, total)


def on_device(
    tok_ids,
    accept,
    sub_ids,
    cache_len,
    spill,
    embed,
    attn_gain,
    w_query,
    w_key,
    w_value,
    w_out,
    mlp_gain,
    w_gate,
    w_up,
    w_down,
    cache_keys,
    cache_values,
):
    block = tok_ids.shape[0]
    slots = cache_keys.shape[0]
    local_vocab = embed.shape[0]
    query_local = w_query.shape[1] // HD
    stored_local = w_key.shape[1] // HD
    per_stored = query_local // stored_local
    group_index = lax.axis_index("grp")
    shard_index = lax.axis_index("tp")
    own_count = cache_len[group_index] - spill[group_index]
    far_count = spill[group_index]
    positions = cache_len[group_index] + jnp.arange(block, dtype=jnp.int32)
    slot_ids = jnp.arange(slots, dtype=jnp.int32)
    tail_ids = slot_ids[block:]
    store_keys = cache_keys.reshape(slots, stored_local, HD)
    store_values = cache_values.reshape(slots, stored_local, HD)
    block_valid = jnp.ones((block,), dtype=bool)
    second_ids = jnp.where(accept == 1, sub_ids, tok_ids)
    vocab_base = group_index * local_vocab
    vocab_ids = jnp.arange(local_vocab, dtype=jnp.int32)

    def lookup(id_list):
        onehot = (id_list[:, None] - vocab_base == vocab_ids[None, :]).astype(jnp.bfloat16)
        return jnp.dot(onehot, embed, preferred_element_type=jnp.float32)

    all_first, all_second = (
        lax.all_gather(tok_ids, "grp", axis=0, tiled=True),
        lax.all_gather(second_ids, "grp", axis=0, tiled=True),
    )
    first_rows = lax.psum_scatter(
        lookup(all_first).astype(jnp.bfloat16), "grp", scatter_dimension=0, tiled=True
    )
    second_rows = lax.psum_scatter(
        lookup(all_second).astype(jnp.bfloat16), "grp", scatter_dimension=0, tiled=True
    )
    tail_keys, tail_values = swapped((cache_keys[block:], cache_values[block:]), "grp", 0)
    far_keys = tail_keys.reshape(slots - block, stored_local, HD)
    far_values = tail_values.reshape(slots - block, stored_local, HD)
    far_valid = tail_ids >= slots - far_count

    def denoise(x_part):
        width = x_part.shape[1]
        x_full = lax.all_gather(x_part, "tp", axis=1, tiled=True)
        normed = rms_normed(x_full.astype(jnp.float32), attn_gain)
        query = rotate(
            jnp.dot(normed, w_query, preferred_element_type=jnp.float32).reshape(
                block, query_local, HD
            ),
            positions,
        )
        query = query.astype(jnp.bfloat16).reshape(block, stored_local, per_stored, HD)
        new_keys = rotate(
            jnp.dot(normed, w_key, preferred_element_type=jnp.float32).reshape(
                block, stored_local, HD
            ),
            positions,
        ).astype(jnp.bfloat16)
        new_values = (
            jnp.dot(normed, w_value, preferred_element_type=jnp.float32)
            .reshape(block, stored_local, HD)
            .astype(jnp.bfloat16)
        )
        own_valid = slot_ids < own_count
        keys = jnp.concatenate([store_keys, far_keys, new_keys], axis=0)
        values = jnp.concatenate([store_values, far_values, new_values], axis=0)
        valid = jnp.concatenate([own_valid, far_valid, block_valid])
        weighted, top, total = partial_attention(query, keys, values, valid)
        attended = weighted / total[..., None]
        mixed = attended.reshape(block, query_local * HD).astype(jnp.bfloat16)
        head_term = jnp.dot(mixed, w_out, preferred_element_type=jnp.float32)
        head_sum = lax.psum(head_term.astype(jnp.bfloat16), "tp").astype(jnp.float32)
        resid_full = (x_full.astype(jnp.float32) + head_sum).astype(jnp.bfloat16)
        resid_part = lax.dynamic_slice_in_dim(resid_full, shard_index * width, width, 1)
        normed_mlp = rms_normed(resid_full.astype(jnp.float32), mlp_gain)
        gate = jnp.dot(normed_mlp, w_gate, preferred_element_type=jnp.float32)
        lift = jnp.dot(normed_mlp, w_up, preferred_element_type=jnp.float32)
        hidden = (jax.nn.silu(gate) * lift).astype(jnp.bfloat16)
        down_term = jnp.dot(hidden, w_down, preferred_element_type=jnp.float32)
        down_part = lax.psum_scatter(
            down_term.astype(jnp.bfloat16), "tp", scatter_dimension=1, tiled=True
        ).astype(jnp.float32)
        return (resid_part.astype(jnp.float32) + down_part).astype(jnp.bfloat16)

    return (denoise(first_rows), denoise(second_rows))


def solution(mesh):
    placed = (
        P("grp"),
        P("grp"),
        P("grp"),
        P(),
        P(),
        P("grp", "tp"),
        P(),
        P(None, "tp"),
        P(None, "tp"),
        P(None, "tp"),
        P("tp", None),
        P(),
        P(None, "tp"),
        P(None, "tp"),
        P("tp", None),
        P("grp", "tp"),
        P("grp", "tp"),
    )
    return jax.shard_map(
        on_device,
        mesh=mesh,
        in_specs=placed,
        out_specs=(P("grp", "tp"), P("grp", "tp")),
        check_vma=False,
    )
```

profile of v0, /device:TPU:72, one launch (start us, length us, event | category | flops | bytes accessed | tf_op | source)
XLA Modules:
  0.0 957.1 jit_solution(10995285730689573226)
XLA Ops:
  8.1 32.7 %all-gather.1 = s32[32,1,256]{2,1,0:T(1,128)S(1)} all-gather(s32[1,1,256]{2,1,0:T(1,128)S(1)} %bitcast.193), channel_id=1, replica_groups=mesh['grp'=32,'tp'=8] {'grp'}, dimensions={0}, use_global_device_ids=true | all-gather | bytes 33792 | tf_op jit(solution)/shard_map/all_gather | solution.py:93
  40.8 37.3 %all-gather = s32[32,1,256]{2,1,0:T(1,128)S(1)} all-gather(s32[1,1,256]{2,1,0:T(1,128)} %bitcast.192), channel_id=1, replica_groups=mesh['grp'=32,'tp'=8] {'grp'}, dimensions={0}, use_global_device_ids=true | all-gather | bytes 33792 | tf_op jit(solution)/shard_map/all_gather | solution.py:92
  78.2 6.3 fusion.10
  85.4 5.4 fusion.11
  90.9 128.5 %reduce-scatter.9.cloned.1.call-done = bf16[256,256]{1,0:T(8,128)(2,1)} async-done(((bf16[8192,256]{1,0:T(8,128)(2,1)}), bf16[256,256]{1,0:T(8,128)(2,1)}) %reduce-scatter.9.cloned.1.call-update) | async-done | bytes 131088 | tf_op jit(solution)/shard_map/reduce_scatter | solution.py:98
  219.5 152.2 %reduce-scatter.5.cloned.1.call-done = bf16[256,256]{1,0:T(8,128)(2,1)} async-done(((bf16[8192,256]{1,0:T(8,128)(2,1)}), bf16[256,256]{1,0:T(8,128)(2,1)}) %reduce-scatter.5.cloned.1.call-update) | async-done | bytes 131088 | tf_op jit(solution)/shard_map/reduce_scatter | solution.py:95
  372.4 2.0 collective-permute-start.1
  374.4 1.6 slice.33
  380.1 77.7 %all-gather.7.cloned.1.call-done = bf16[256,2048]{1,0:T(8,128)(2,1)} async-done(((bf16[256,256]{1,0:T(8,128)(2,1)}), bf16[256,2048]{1,0:T(8,128)(2,1)}) %all-gather.7.cloned.1.call-update) | async-done | bytes 1048592 | tf_op jit(solution)/shard_map/all_gather | solution.py:108
  457.8 1.5 fusion.34
  459.3 58.2 %all-gather.5.cloned.1.call-done = bf16[256,2048]{1,0:T(8,128)(2,1)} async-done(((bf16[256,256]{1,0:T(8,128)(2,1)}), bf16[256,2048]{1,0:T(8,128)(2,1)}) %all-gather.5.cloned.1.call-update) | async-done | bytes 1048592 | tf_op jit(solution)/shard_map/all_gather | solution.py:108
  517.5 1.7 fusion.30
  519.2 2.3 fusion.114
  523.5 8.1 fusion.61
  531.7 14.5 %bitcast_reduce_fusion = (f32[256,4]{0,1:T(4,128)S(1)}, f32[256,4]{0,1:T(4,128)S(1)}, f32[4096,256,4]{1,0,2:T(8,128)}) fusion(pred[4096]{0:T(1024)(128)(4,1)S(1)} %pad_add_fusion, f32[4096,256,4]{1,0,2:T(8,128)} %fusion.61, bf16[256,4,32]{0,2,1:T(8,128)(2,1)S(1)} %get-tuple-element.13, bf16[256,4,32]{0,2,1:T(8,128)(2,1)S(1)} %get-tuple-element.12, ...), kind=kOutput, calls=%fused_computation.1 | convolution fusion | flops 564393984 | bytes 34222080 | tf_op jit(solution)/shard_map/bcgd,kcd->bcgk/dot_general | solution.py:37
  546.2 14.2 %fusion.8 = (f32[256,4]{0,1:T(4,128)S(1)}, f32[256,4]{0,1:T(4,128)S(1)}) fusion(f32[4096,256,4]{1,0,2:T(8,128)} %get-tuple-element.26, f32[256,4]{0,1:T(4,128)S(1)} %get-tuple-element.4, pred[4096]{0:T(1024)(128)(4,1)S(1)} %pad_add_fusion, f32[256,4]{0,1:T(4,128)S(1)} %get-tuple-element.5, f32[4096,256,4]{1,0,2:T(8,128)} %fusion.61), kind=kLoop, calls=%fused_computation.16 | loop fusion | flops 41940992 | bytes 33574912 | tf_op jit(solution)/shard_map/reduce_sum | solution.py:41
  561.0 5.4 fusion.51
  566.5 1.5 convolution_convert_fusion.3
  568.5 5.1 fusion.57
  573.6 1.5 convolution_convert_fusion.1
  575.4 188.3 %all-reduce.3.cloned.1.call-done = (bf16[256,2048]{1,0:T(8,128)(2,1)}, bf16[256,2048]{1,0:T(8,128)(2,1)}) async-done(((bf16[256,2048]{1,0:T(8,128)(2,1)}, bf16[256,2048]{1,0:T(8,128)(2,1)}), (bf16[256,2048]{1,0:T(8,128)(2,1)}, bf16[256,2048]{1,0:T(8,128)(2,1)})) %all-reduce.3.cloned.1.call-update) | async-done | bytes 2097168 | tf_op jit(solution)/shard_map/psum | solution.py:136
  763.7 2.2 fusion.24
  766.0 1.0 copy-done.4
  767.0 1.9 fusion.78
  768.9 6.6 convolution_convert_fusion.2
  775.6 2.2 fusion.27
  778.8 1.9 fusion.74
  780.8 6.6 convolution_convert_fusion
  787.4 73.9 %reduce-scatter.7.cloned.1.call-done = bf16[256,256]{1,0:T(8,128)(2,1)} async-done(((bf16[256,2048]{1,0:T(8,128)(2,1)}), bf16[256,256]{1,0:T(8,128)(2,1)}) %reduce-scatter.7.cloned.1.call-update) | async-done | bytes 131088 | tf_op jit(solution)/shard_map/reduce_scatter | solution.py:144
  861.3 1.7 add_convert_fusion.1
  863.0 85.6 %reduce-scatter.11.cloned.1.call-done = bf16[256,256]{1,0:T(8,128)(2,1)} async-done(((bf16[256,2048]{1,0:T(8,128)(2,1)}), bf16[256,256]{1,0:T(8,128)(2,1)}) %reduce-scatter.11.cloned.1.call-update) | async-done | bytes 131088 | tf_op jit(solution)/shard_map/reduce_scatter | solution.py:144
  948.6 1.7 add_convert_fusion
  (93 shorter events, 9.3 us)
Async XLA Ops:
  7.2 761.7 %copy-start = (bf16[704,2048]{1,0:T(8,128)(2,1)S(1)}, bf16[704,2048]{1,0:T(8,128)(2,1)}, u32[]{:S(2)}) copy-start(bf16[704,2048]{1,0:T(8,128)(2,1)} %param.31) | copy-start | bytes 8650756
  7.2 212.2 %reduce-scatter.9.cloned.1.call-start = ((), (), s32[]{:S(2)}) async-start(), calls=%async_computation.7 | async-start | bytes 4325376 | tf_op jit(solution)/shard_map/reduce_scatter | solution.py:98
  84.4 287.2 %reduce-scatter.5.cloned.1.call-start = ((), (), s32[]{:S(2)}) async-start(), calls=%async_computation.4 | async-start | bytes 4325376 | tf_op jit(solution)/shard_map/reduce_scatter | solution.py:95
  90.8 280.9 %copy-start.6 = (bf16[2048,64]{0,1:T(8,128)(2,1)S(1)}, bf16[2048,64]{0,1:T(8,128)(2,1)}, u32[]{:S(2)}) copy-start(bf16[2048,64]{0,1:T(8,128)(2,1)} %param.32) | copy-start | bytes 786436
  90.8 285.2 %copy-start.16 = (s32[32]{0:T(128)S(1)}, s32[32]{0:T(128)}, u32[]{:S(2)}) copy-start(s32[32]{0:T(128)} %param.20) | copy-start | bytes 388
  90.8 285.8 %copy-start.17 = (s32[32]{0:T(128)S(1)}, s32[32]{0:T(128)}, u32[]{:S(2)}) copy-start(s32[32]{0:T(128)} %param.21) | copy-start | bytes 388
  90.8 428.3 %copy-start.14 = (f32[2048]{0:T(1024)S(1)}, f32[2048]{0:T(1024)}, u32[]{:S(2)}) copy-start(f32[2048]{0:T(1024)} %param.23) | copy-start | bytes 24580
  90.9 366.9 %all-gather.7.cloned.1.call-start = ((), (), s32[]{:S(2)}) async-start(), calls=%async_computation.8 | async-start | bytes 1179648 | tf_op jit(solution)/shard_map/all_gather | solution.py:108
  219.4 298.0 %all-gather.5.cloned.1.call-start = ((), (), s32[]{:S(2)}) async-start(), calls=%async_computation.5 | async-start | bytes 1179648 | tf_op jit(solution)/shard_map/all_gather | solution.py:108
  371.7 392.1 %all-reduce.3.cloned.1.call-start = ((), (), s32[]{:S(2)}) async-start(), calls=%async_computation.10 | async-start | bytes 4194304 | tf_op jit(solution)/shard_map/psum | solution.py:136
  372.4 151.1 %collective-permute-start.1 = (bf16[1792,64]{0,1:T(8,128)(2,1)}, bf16[1792,64]{0,1:T(8,128)(2,1)S(1)}, u32[]{:S(2)}, u32[]{:S(2)}) collective-permute-start(bf16[1792,64]{0,1:T(8,128)(2,1)} %slice.35), channel_id=1, source_target_pairs={{0,8},{8,0},{16,24},{24,16},{32,40},{40,32},{48,56},{56,48},{64,72... | collective-permute-start | bytes 688136 | tf_op jit(solution)/shard_map/ppermute | solution.py:14
  376.0 184.9 %collective-permute-start = (bf16[1792,64]{0,1:T(8,128)(2,1)}, bf16[1792,64]{0,1:T(8,128)(2,1)}, u32[]{:S(2)}, u32[]{:S(2)}) collective-permute-start(bf16[1792,64]{0,1:T(8,128)(2,1)} %slice.33), channel_id=1, source_target_pairs={{0,8},{8,0},{16,24},{24,16},{32,40},{40,32},{48,56},{56,48},{64,72... | collective-permute-start | bytes 688136 | tf_op jit(solution)/shard_map/ppermute | solution.py:14
  517.5 4.0 copy-start.3
  517.5 4.0 copy-start.10
  519.1 3.1 copy-start.2
  519.1 3.1 copy-start.12
  531.6 29.3 %slice-start = ((s8[16777216]{0:T(1024)(128)(4,1)}), s8[4194304]{0:T(1024)(128)(4,1)S(1)}, s32[]{:S(2)}) async-start(s8[16777216]{0:T(1024)(128)(4,1)} %bitcast.174), calls=%async_computation.11 | async-start | bytes 8388608
  531.7 29.3 %slice-start.1 = ((s8[16777216]{0:T(1024)(128)(4,1)}), s8[4194304]{0:T(1024)(128)(4,1)S(1)}, s32[]{:S(2)}) async-start(s8[16777216]{0:T(1024)(128)(4,1)} %bitcast.174), calls=%async_computation.12 | async-start | bytes 8388608
  531.7 29.3 %slice-start.2 = ((s8[16777216]{0:T(1024)(128)(4,1)}), s8[4194304]{0:T(1024)(128)(4,1)S(1)}, s32[]{:S(2)}) async-start(s8[16777216]{0:T(1024)(128)(4,1)} %bitcast.174), calls=%async_computation.13 | async-start | bytes 8388608
  546.2 14.2 %copy-start.13 = (bf16[2048,64]{0,1:T(8,128)(2,1)S(1)}, bf16[2048,64]{0,1:T(8,128)(2,1)}, u32[]{:S(2)}) copy-start(bf16[2048,64]{0,1:T(8,128)(2,1)} %param.26) | copy-start | bytes 786436
  546.2 14.8 %slice-start.3 = ((s8[16777216]{0:T(1024)(128)(4,1)}), s8[4194304]{0:T(1024)(128)(4,1)S(1)}, s32[]{:S(2)}) async-start(s8[16777216]{0:T(1024)(128)(4,1)} %bitcast.174), calls=%async_computation.14 | async-start | bytes 8388608
  546.2 14.8 %copy-start.7 = (bf16[2048,64]{0,1:T(8,128)(2,1)S(1)}, bf16[2048,64]{0,1:T(8,128)(2,1)}, u32[]{:S(2)}) copy-start(bf16[2048,64]{0,1:T(8,128)(2,1)} %param.33) | copy-start | bytes 786436
  560.4 8.1 slice-start.4
  561.0 5.5 copy-start.1
  561.0 7.5 slice-start.5
  561.0 7.5 slice-start.6
  561.0 7.5 slice-start.7
  575.1 191.9 %copy-start.15 = (f32[2048]{0:T(1024)S(1)}, f32[2048]{0:T(1024)}, u32[]{:S(2)}) copy-start(f32[2048]{0:T(1024)} %param.28) | copy-start | bytes 24580
  575.1 286.2 %reduce-scatter.7.cloned.1.call-start = ((), (), s32[]{:S(2)}) async-start(), calls=%async_computation.6 | async-start | bytes 1179648 | tf_op jit(solution)/shard_map/reduce_scatter | solution.py:144
  763.7 3.2 copy-start.8
  775.6 173.0 %reduce-scatter.11.cloned.1.call-start = ((), (), s32[]{:S(2)}) async-start(), calls=%async_computation.9 | async-start | bytes 1179648 | tf_op jit(solution)/shard_map/reduce_scatter | solution.py:144
  775.6 3.2 copy-start.9
  (3 other events, 2.9 us)
Sparse Core Ops, SparseCore 0:
  84.6 134.7 reduce-scatter.8
  221.9 149.6 reduce-scatter.4
  374.1 83.5 all-gather.6
  460.1 57.3 all-gather.4
  575.2 188.4 all-reduce.2
  775.7 85.5 reduce-scatter.6
  865.8 82.7 reduce-scatter.10
where the time goes:
time: 961 us; the launch traced here: 957 us
  waiting for transfers between devices  765 us (80%)
  blocking collectives  70.1 us (7%)
  matrix products  70 us (7%)
  other arithmetic  27.1 us (3%)
  between operations  16.5 us (2%)
    psum x1, waiting for transfers between devices, denoise(): lax.psum(head_term.astype(jnp.bfloat16), 'tp').astype(jnp.float32)  188 us
    reduce_scatter x2, waiting for transfers between devices, denoise(): lax.psum_scatter(down_term.astype(jnp.bfloat16), 'tp', scatter_dimension=...  160 us
    reduce_scatter x1, waiting for transfers between devices, on_device(): lax.psum_scatter(lookup(all_first).astype(jnp.bfloat16), 'grp', scatter_d...  152 us
    all_gather x2, waiting for transfers between devices, denoise(): x_full = lax.all_gather(x_part, 'tp', axis=1, tiled=True)  136 us
    reduce_scatter x1, waiting for transfers between devices, on_device(): lax.psum_scatter(lookup(all_second).astype(jnp.bfloat16), 'grp', scatter_...  128 us
    all_gather x1, blocking collectives, on_device(): lax.all_gather(tok_ids, 'grp', axis=0, tiled=True)  37.3 us
    all_gather x1, blocking collectives, on_device(): lax.all_gather(second_ids, 'grp', axis=0, tiled=True)  32.7 us
    dot_general x2, matrix products, partial_attention(): jnp.einsum('bcgd,kcd->bcgk', query, keys, preferred_element_type=jnp.floa...  22.6 us
  transfers between devices with their start and end apart: 9, of which 7 were waited for; matrix products, arithmetic and copies ran while one was open for 7% of the time, Pallas kernels for 0%

commit v1 on v0

v1 whole, which is shorter than its diff:
```python
import jax
import jax.numpy as jnp
from jax import lax
from jax.sharding import PartitionSpec as P

HD = 64


EPSILON = 1e-05
SENTINEL = -1e30


def shifted(array, axis, step):
    n = lax.axis_size(axis)
    return lax.ppermute(array, axis, [(i, (i + step) % n) for i in range(n)])


def swapped(array, axis, bit):
    return lax.ppermute(array, axis, [(i, i ^ 1 << bit) for i in range(lax.axis_size(axis))])


def tp_gather(part):
    rows, width = part.shape
    n_x = lax.axis_size("tp") // 2
    me = lax.axis_index("tp")
    mine_x = me // 2
    partner = swapped(part, "tp", 0)
    low_first = me % 2 == 0
    pair = jnp.stack([jnp.where(low_first, part, partner), jnp.where(low_first, partner, part)])
    received = [pair] + [shifted(pair, "tp", 2 * k) for k in range(1, n_x)]
    stacked = jnp.stack(received)
    order = (mine_x - jnp.arange(n_x, dtype=jnp.int32)) % n_x
    full = jnp.take(stacked, order, axis=0)
    return full.transpose(2, 0, 1, 3).reshape(rows, n_x * 2 * width)


def tp_reduce(full):
    rows, total_width = full.shape
    n_x = lax.axis_size("tp") // 2
    me = lax.axis_index("tp")
    mine_x = me // 2
    pieces = full.reshape(rows, n_x, total_width // n_x)
    acc = jnp.take(pieces, mine_x, axis=1).astype(jnp.float32)
    for k in range(1, n_x):
        piece = jnp.take(pieces, (mine_x + k) % n_x, axis=1)
        acc = acc + shifted(piece, "tp", 2 * k).astype(jnp.float32)
    halves = acc.reshape(rows, 2, total_width // n_x // 2)
    low = me % 2 == 0
    mine = jnp.where(low, halves[:, 0], halves[:, 1])
    other = jnp.where(low, halves[:, 1], halves[:, 0])
    got = swapped(other.astype(jnp.bfloat16), "tp", 0)
    return mine + got.astype(jnp.float32)


def rms_normed(values, gain):
    square = jnp.mean(values * values, axis=-1, keepdims=True)
    return (values * lax.rsqrt(square + EPSILON) * gain).astype(jnp.bfloat16)


def rotate(vectors, positions):
    half = vectors.shape[-1] // 2
    exponent = jnp.arange(half, dtype=jnp.float32) * (-2.0 / vectors.shape[-1])
    freqs = jnp.power(jnp.float32(10000.0), exponent)
    angles = positions.astype(jnp.float32)[:, None] * freqs[None, :]
    cosine = jnp.cos(angles)[:, None, :]
    sine = jnp.sin(angles)[:, None, :]
    first = vectors[..., :half]
    second = vectors[..., half:]
    return jnp.concatenate(
        [first * cosine - second * sine, second * cosine + first * sine], axis=-1
    )


def partial_attention(query, keys, values, valid):
    scores = jnp.einsum("pbcgd,pkcd->pbcgk", query, keys, preferred_element_type=jnp.float32) * 0.125
    scores = jnp.where(valid, scores, SENTINEL)
    top = jnp.max(scores, axis=-1)
    weights = jnp.where(valid, jnp.exp(scores - top[..., None]), 0.0)
    total = jnp.sum(weights, axis=-1)
    weighted = jnp.einsum(
        "pbcgk,pkcd->pbcgd", weights.astype(jnp.bfloat16), values, preferred_element_type=jnp.float32
    )
    return (weighted, top, total)


def on_device(
    tok_ids,
    accept,
    sub_ids,
    cache_len,
    spill,
    embed,
    attn_gain,
    w_query,
    w_key,
    w_value,
    w_out,
    mlp_gain,
    w_gate,
    w_up,
    w_down,
    cache_keys,
    cache_values,
):
    block = tok_ids.shape[0]
    slots = cache_keys.shape[0]
    query_local = w_query.shape[1] // HD
    stored_local = w_key.shape[1] // HD
    per_stored = query_local // stored_local
    group_index = lax.axis_index("grp")
    own_count = cache_len[group_index] - spill[group_index]
    far_count = spill[group_index]
    positions = cache_len[group_index] + jnp.arange(block, dtype=jnp.int32)
    slot_ids = jnp.arange(slots, dtype=jnp.int32)
    tail_ids = slot_ids[block:]
    store_keys = cache_keys.reshape(slots, stored_local, HD)
    store_values = cache_values.reshape(slots, stored_local, HD)
    second_ids = jnp.where(accept == 1, sub_ids, tok_ids)

    table = lax.all_gather(embed, "grp", axis=0, tiled=True)
    both_ids = jnp.concatenate([tok_ids, second_ids])
    x_part = jnp.take(table, both_ids, axis=0)
    rows, width = x_part.shape

    tail_keys, tail_values = swapped((cache_keys[block:], cache_values[block:]), "grp", 0)
    far_keys = tail_keys.reshape(slots - block, stored_local, HD)
    far_values = tail_values.reshape(slots - block, stored_local, HD)
    far_valid = tail_ids >= slots - far_count
    own_valid = slot_ids < own_count
    valid = jnp.concatenate([own_valid, far_valid, jnp.ones((block,), dtype=bool)])

    x_full = tp_gather(x_part)
    normed = rms_normed(x_full.astype(jnp.float32), attn_gain)
    both_positions = jnp.concatenate([positions, positions])
    query = rotate(
        jnp.dot(normed, w_query, preferred_element_type=jnp.float32).reshape(
            rows, query_local, HD
        ),
        both_positions,
    )
    query = query.astype(jnp.bfloat16).reshape(2, block, stored_local, per_stored, HD)
    new_keys = rotate(
        jnp.dot(normed, w_key, preferred_element_type=jnp.float32).reshape(
            rows, stored_local, HD
        ),
        both_positions,
    ).astype(jnp.bfloat16).reshape(2, block, stored_local, HD)
    new_values = (
        jnp.dot(normed, w_value, preferred_element_type=jnp.float32)
        .reshape(2, block, stored_local, HD)
        .astype(jnp.bfloat16)
    )
    cached_keys = jnp.concatenate([store_keys, far_keys], axis=0)
    cached_values = jnp.concatenate([store_values, far_values], axis=0)
    keys = jnp.concatenate(
        [jnp.broadcast_to(cached_keys[None], (2,) + cached_keys.shape), new_keys], axis=1
    )
    values = jnp.concatenate(
        [jnp.broadcast_to(cached_values[None], (2,) + cached_values.shape), new_values], axis=1
    )
    weighted, top, total = partial_attention(query, keys, values, valid)
    attended = weighted / total[..., None]
    mixed = attended.reshape(rows, query_local * HD).astype(jnp.bfloat16)
    head_term = jnp.dot(mixed, w_out, preferred_element_type=jnp.float32)
    head_sum = tp_reduce(head_term.astype(jnp.bfloat16))
    resid_part = (x_part.astype(jnp.float32) + head_sum).astype(jnp.bfloat16)
    resid_full = tp_gather(resid_part)
    normed_mlp = rms_normed(resid_full.astype(jnp.float32), mlp_gain)
    gate = jnp.dot(normed_mlp, w_gate, preferred_element_type=jnp.float32)
    lift = jnp.dot(normed_mlp, w_up, preferred_element_type=jnp.float32)
    hidden = (jax.nn.silu(gate) * lift).astype(jnp.bfloat16)
    down_term = jnp.dot(hidden, w_down, preferred_element_type=jnp.float32)
    down_part = tp_reduce(down_term.astype(jnp.bfloat16))
    out = (resid_part.astype(jnp.float32) + down_part).astype(jnp.bfloat16)
    return (out[:block], out[block:])


def solution(mesh):
    placed = (
        P("grp"),
        P("grp"),
        P("grp"),
        P(),
        P(),
        P("grp", "tp"),
        P(),
        P(None, "tp"),
        P(None, "tp"),
        P(None, "tp"),
        P("tp", None),
        P(),
        P(None, "tp"),
        P(None, "tp"),
        P("tp", None),
        P("grp", "tp"),
        P("grp", "tp"),
    )
    return jax.shard_map(
        on_device,
        mesh=mesh,
        in_specs=placed,
        out_specs=(P("grp", "tp"), P("grp", "tp")),
        check_vma=False,
    )
```

time: 961 us -> 444 us (0.46)
  the two profiles are of different devices: /device:TPU:72 before, /device:TPU:32 now
where the time goes in v1:
time: 444 us; the launch traced here: 436 us
  waiting for transfers between devices  189 us (43%)
  local copies, waits for them, and re-layouts  96.7 us (22%)
  other arithmetic  59.6 us (13%)
  matrix products  44.6 us (10%)
  starting transfers between devices  29.5 us (7%)
  between operations  16.9 us (4%)
    ppermute x12, waiting for transfers between devices, shifted(): return lax.ppermute(array, axis, [(i, (i + step) % n) for i in range(n)])  86.6 us
    all_gather x1, waiting for transfers between devices, on_device(): table = lax.all_gather(embed, 'grp', axis=0, tiled=True)  61.4 us
    ppermute x6, waiting for transfers between devices, swapped(): lax.ppermute(array, axis, [(i, i ^ 1 << bit) for i in range(lax.axis_size...  40.3 us
    convert_element_type x3, local copies, waits for them, and re-layouts, on_device(): normed = rms_normed(x_full.astype(jnp.float32), attn_gain)  19.3 us
    ppermute x12, starting transfers between devices, shifted(): return lax.ppermute(array, axis, [(i, (i + step) % n) for i in range(n)])  17.9 us
    another operation x2, local copies, waits for them, and re-layouts, tp_reduce(): acc = jnp.take(pieces, mine_x, axis=1).astype(jnp.float32)  17.1 us
    dot_general x1, matrix products, partial_attention(): jnp.einsum('pbcgk,pkcd->pbcgd', weights.astype(jnp.bfloat16), values, pre...  15.7 us
    reduce_sum x1, other arithmetic, partial_attention(): total = jnp.sum(weights, axis=-1)  15.6 us
  transfers between devices with their start and end apart: 19, of which 14 were waited for; matrix products, arithmetic and copies ran while one was open for 6% of the time, Pallas kernels for 0%

profile of v1, /device:TPU:32, one launch (start us, length us, event | category | flops | bytes accessed | tf_op | source)
XLA Modules:
  0.0 436.3 jit_solution(2578726305064428950)
XLA Ops:
  20.3 61.4 %all-gather.2.cloned.1.call-done = bf16[16384,256]{1,0:T(8,128)(2,1)} async-done(((bf16[512,256]{1,0:T(8,128)(2,1)}), bf16[16384,256]{1,0:T(8,128)(2,1)}) %all-gather.2.cloned.1.call-update) | async-done | bytes 8388624 | tf_op jit(solution)/shard_map/all_gather | solution.py:120
  81.7 6.0 %gather_fusion = bf16[512,256]{1,0:T(8,128)(2,1)S(1)} fusion(bf16[16384,256]{1,0:T(8,128)(2,1)} %all-gather.2.cloned.1.call-done, s32[1024]{0:T(1024)S(1)} %pad_clamp_fusion.1), kind=kCustom, calls=%fused_computation.2 | custom fusion | bytes 526336 | tf_op jit(solution)/shard_map/jit(_take)/gather | solution.py:122
  88.6 3.6 collective-permute-start.1
  96.8 10.1 %collective-permute-done.1 = bf16[512,256]{1,0:T(8,128)(2,1)} collective-permute-done((bf16[512,256]{1,0:T(8,128)(2,1)}, bf16[512,256]{1,0:T(8,128)(2,1)}, u32[]{:S(2)}, u32[]{:S(2)}) %collective-permute-start.1) | collective-permute-done | bytes 262176 | tf_op jit(solution)/shard_map/ppermute | solution.py:19
  117.2 7.4 %collective-permute-done.3 = bf16[2,512,256]{2,1,0:T(8,128)(2,1)S(1)} collective-permute-done((bf16[2,512,256]{2,1,0:T(8,128)(2,1)S(1)}, bf16[2,512,256]{2,1,0:T(8,128)(2,1)S(1)}, u32[]{:S(2)}, u32[]{:S(2)}) %collective-permute-start.3) | collective-permute-done | bytes 524320 | tf_op jit(solution)/shard_map/ppermute | solution.py:15
  124.6 9.6 %collective-permute-done.2 = bf16[2,512,256]{2,1,0:T(8,128)(2,1)S(1)} collective-permute-done((bf16[2,512,256]{2,1,0:T(8,128)(2,1)S(1)}, bf16[2,512,256]{2,1,0:T(8,128)(2,1)S(1)}, u32[]{:S(2)}, u32[]{:S(2)}) %collective-permute-start.2) | collective-permute-done | bytes 524320 | tf_op jit(solution)/shard_map/ppermute | solution.py:15
  135.8 3.7 gather_fusion.1
  144.3 5.4 %copy.32 = f32[512,4,2,256]{0,3,2,1:T(8,128)} copy(f32[512,4,2,256]{3,0,2,1:T(8,128)} %convert_bitcast_fusion) | data formatting | bytes 8388608 | tf_op jit(solution)/shard_map/convert_element_type | solution.py:133
  149.8 7.4 %copy.31 = f32[512,4,2,256]{3,2,1,0:T(2,128)} copy(f32[512,4,2,256]{3,0,2,1:T(8,128)} %convert_bitcast_fusion) | data formatting | bytes 8388608 | tf_op jit(solution)/shard_map/convert_element_type | solution.py:133
  157.8 3.6 fusion.18
  161.4 4.2 copy.35
  169.8 6.4 %reshape.510 = f32[2,256,2048]{2,1,0:T(8,128)} reshape(f32[512,4,2,256]{3,2,1,0:T(2,128)} %copy.31) | data formatting | bytes 8388608 | tf_op jit(solution)/shard_map/convert_element_type | solution.py:133
  179.1 12.5 %bitcast_reduce_fusion = (f32[2,256,4]{1,2,0:T(4,128)S(1)}, f32[2,4096,256,4]{2,1,3,0:T(8,128)}) fusion(pred[4096]{0:T(1024)(128)(4,1)S(1)} %pad_add_fusion, bf16[2,256,4,32]{1,3,2,0:T(8,128)(2,1)S(1)} %get-tuple-element.45, bf16[2,256,4,32]{1,3,2,0:T(8,128)(2,1)S(1)} %get-tuple-element.46, bf16[2,256,1,32]{1,3,0,2:T(8,128)(2,1)S(1)} %get-tuple-element.47, ...), kind=kOutput, calls=%fused_computation.4 | convolution fusion | flops 1102575616 | bytes 34877440 | tf_op jit(solution)/shard_map/pbcgd,pkcd->pbcgk/dot_general | solution.py:75
  191.6 15.6 %fusion.2 = f32[2,256,4]{1,2,0:T(4,128)S(1)} fusion(f32[2,4096,256,4]{2,1,3,0:T(8,128)} %get-tuple-element.44, f32[2,256,4]{1,2,0:T(4,128)S(1)} %get-tuple-element.43, pred[4096]{0:T(1024)(128)(4,1)S(1)} %pad_add_fusion), kind=kLoop, calls=%fused_computation.8 | loop fusion | flops 41940992 | bytes 33574912 | tf_op jit(solution)/shard_map/reduce_sum | solution.py:79
  208.2 15.7 %fusion.33 = bf16[2,256,1,4,64]{1,4,3,0,2:T(8,128)(2,1)S(1)} fusion(f32[2,4096,256,4]{2,1,3,0:T(8,128)} %get-tuple-element.44, f32[2,256,4]{1,2,0:T(4,128)S(1)} %get-tuple-element.43, pred[4096]{0:T(1024)(128)(4,1)S(1)} %pad_add_fusion, bf16[2,256,1,64]{1,3,0,2:T(8,128)(2,1)S(1)} %fusion.26, bf16[2,3840,1,64]{1,3,0,2:T(8,128)(2,1)S(1)} %broadcast_in_dim.78, ...), kind=kOutput, calls=%fused_computation.48 | convolution fusion | flops 1118044160 | bytes 34885632 | tf_op jit(solution)/shard_map/pbcgk,pkcd->pbcgd/dot_general | solution.py:80
  226.3 4.5 %reshape.399 = bf16[512,4,512]{2,1,0:T(4,128)(2,1)} reshape(bf16[512,2048]{1,0:T(8,128)(2,1)} %convolution_convert_fusion) | data formatting | bytes 4194304 | tf_op jit(solution)/shard_map/reshape | solution.py:42
  230.8 9.0 %constant_dynamic-slice_fusion.6 = (bf16[512,1,512]{2,1,0:T(2,128)(2,1)}, bf16[512,1,512]{2,1,0:T(2,128)(2,1)S(1)}, bf16[512,1,512]{2,1,0:T(2,128)(2,1)S(1)}, bf16[512,1,512]{2,1,0:T(2,128)(2,1)S(1)}) fusion(bf16[512,4,512]{2,1,0:T(4,128)(2,1)} %reshape.399, s32[]{:T(128)S(6)} %select_n.207, s32[]{:T(128)S(6)} %select_n.211, s32[]{:T(128)S(6)} %select_n.209, ...), kind=kLoop, calls=%fused_computation.136 | loop fusion | bytes 4194320 | tf_op jit(solution)/shard_map/jit(_take) | solution.py:43
  245.9 19.3 %collective-permute-done.8 = bf16[512,512]{1,0:T(8,128)(2,1)} collective-permute-done((bf16[512,512]{1,0:T(8,128)(2,1)S(1)}, bf16[512,512]{1,0:T(8,128)(2,1)}, u32[]{:S(2)}, u32[]{:S(2)}) %collective-permute-start.8) | collective-permute-done | bytes 524320 | tf_op jit(solution)/shard_map/ppermute | solution.py:15
  265.2 4.6 %collective-permute-done.6 = bf16[512,512]{1,0:T(8,128)(2,1)} collective-permute-done((bf16[512,512]{1,0:T(8,128)(2,1)}, bf16[512,512]{1,0:T(8,128)(2,1)}, u32[]{:S(2)}, u32[]{:S(2)}) %collective-permute-start.6) | collective-permute-done | bytes 524320 | tf_op jit(solution)/shard_map/ppermute | solution.py:15
  284.6 11.6 %collective-permute-done.9 = bf16[512,256]{1,0:T(8,128)(2,1)S(1)} collective-permute-done((bf16[512,256]{1,0:T(8,128)(2,1)S(1)}, bf16[512,256]{1,0:T(8,128)(2,1)S(1)}, u32[]{:S(2)}, u32[]{:S(2)}) %collective-permute-start.9) | collective-permute-done | bytes 262176 | tf_op jit(solution)/shard_map/ppermute | solution.py:19
  297.3 3.8 collective-permute-start.10
  301.1 9.2 %collective-permute-done.10 = bf16[512,256]{1,0:T(8,128)(2,1)S(1)} collective-permute-done((bf16[512,256]{1,0:T(8,128)(2,1)S(1)}, bf16[512,256]{1,0:T(8,128)(2,1)S(1)}, u32[]{:S(2)}, u32[]{:S(2)}) %collective-permute-start.10) | collective-permute-done | bytes 262176 | tf_op jit(solution)/shard_map/ppermute | solution.py:19
  314.9 12.0 %collective-permute-done.12 = bf16[2,512,256]{2,1,0:T(8,128)(2,1)S(1)} collective-permute-done((bf16[2,512,256]{2,1,0:T(8,128)(2,1)S(1)}, bf16[2,512,256]{2,1,0:T(8,128)(2,1)S(1)}, u32[]{:S(2)}, u32[]{:S(2)}) %collective-permute-start.12) | collective-permute-done | bytes 524320 | tf_op jit(solution)/shard_map/ppermute | solution.py:15
  326.9 10.1 %collective-permute-done.11 = bf16[2,512,256]{2,1,0:T(8,128)(2,1)S(1)} collective-permute-done((bf16[2,512,256]{2,1,0:T(8,128)(2,1)S(1)}, bf16[2,512,256]{2,1,0:T(8,128)(2,1)S(1)}, u32[]{:S(2)}, u32[]{:S(2)}) %collective-permute-start.11) | collective-permute-done | bytes 524320 | tf_op jit(solution)/shard_map/ppermute | solution.py:15
  338.6 3.7 gather_fusion.2
  347.1 5.3 %copy.49 = f32[512,4,2,256]{0,3,2,1:T(8,128)} copy(f32[512,4,2,256]{3,0,2,1:T(8,128)} %convert_bitcast_fusion.1) | data formatting | bytes 8388608 | tf_op jit(solution)/shard_map/convert_element_type | solution.py:168
  359.3 7.6 %convolution_convert_fusion.1 = bf16[512,2048]{1,0:T(8,128)(2,1)} fusion(bf16[704,2048]{1,0:T(8,128)(2,1)S(1)} %copy-done, bf16[2048,704]{0,1:T(8,128)(2,1)} %param.34, bf16[512,2048]{0,1:T(8,128)(2,1)} %copy-done.6, f32[512,704]{0,1:T(8,128)} %fusion.82), kind=kOutput, calls=%fused_computation.31 | convolution fusion | flops 2956001280 | bytes 11403264 | tf_op jit(solution)/shard_map/dot_general | solution.py:172
  366.9 4.5 %reshape.401 = bf16[512,4,512]{2,1,0:T(4,128)(2,1)} reshape(bf16[512,2048]{1,0:T(8,128)(2,1)} %convolution_convert_fusion.1) | data formatting | bytes 4194304 | tf_op jit(solution)/shard_map/reshape | solution.py:42
  371.4 8.1 %constant_dynamic-slice_fusion.1 = (bf16[512,1,512]{2,1,0:T(2,128)(2,1)S(1)}, bf16[512,1,512]{2,1,0:T(2,128)(2,1)S(1)}, bf16[512,1,512]{2,1,0:T(2,128)(2,1)S(1)}, bf16[512,1,512]{2,1,0:T(2,128)(2,1)S(1)}) fusion(bf16[512,4,512]{2,1,0:T(4,128)(2,1)} %reshape.401, s32[]{:T(128)S(6)} %select_n.207, s32[]{:T(128)S(6)} %select_n.211, s32[]{:T(128)S(6)} %select_n.209, ...), kind=kLoop, calls=%fused_computation.131 | loop fusion | bytes 4194320 | tf_op jit(solution)/shard_map/jit(_take) | solution.py:43
  382.9 11.9 %collective-permute-done.16 = bf16[512,512]{1,0:T(8,128)(2,1)S(1)} collective-permute-done((bf16[512,512]{1,0:T(8,128)(2,1)S(1)}, bf16[512,512]{1,0:T(8,128)(2,1)S(1)}, u32[]{:S(2)}, u32[]{:S(2)}) %collective-permute-start.16) | collective-permute-done | bytes 524320 | tf_op jit(solution)/shard_map/ppermute | solution.py:15
  394.7 11.6 %collective-permute-done.14 = bf16[512,512]{1,0:T(8,128)(2,1)S(1)} collective-permute-done((bf16[512,512]{1,0:T(8,128)(2,1)S(1)}, bf16[512,512]{1,0:T(8,128)(2,1)S(1)}, u32[]{:S(2)}, u32[]{:S(2)}) %collective-permute-start.14) | collective-permute-done | bytes 524320 | tf_op jit(solution)/shard_map/ppermute | solution.py:15
  417.9 9.4 %collective-permute-done.17 = bf16[512,256]{1,0:T(8,128)(2,1)S(1)} collective-permute-done((bf16[512,256]{1,0:T(8,128)(2,1)S(1)}, bf16[512,256]{1,0:T(8,128)(2,1)S(1)}, u32[]{:S(2)}, u32[]{:S(2)}) %collective-permute-start.17) | collective-permute-done | bytes 262176 | tf_op jit(solution)/shard_map/ppermute | solution.py:19
  (147 shorter events, 100.5 us)
Async XLA Ops:
  7.2 352.2 %copy-start = (bf16[704,2048]{1,0:T(8,128)(2,1)S(1)}, bf16[704,2048]{1,0:T(8,128)(2,1)}, u32[]{:S(2)}) copy-start(bf16[704,2048]{1,0:T(8,128)(2,1)} %param.35) | copy-start | bytes 8650756
  7.2 85.6 %copy-start.15 = (f32[2048]{0:T(1024)S(1)}, f32[2048]{0:T(1024)}, u32[]{:S(2)}) copy-start(f32[2048]{0:T(1024)} %param.27) | copy-start | bytes 24580
  7.2 74.6 %all-gather.2.cloned.1.call-start = ((), (), s32[]{:S(2)}) async-start(), calls=%async_computation | async-start | bytes 8650752 | tf_op jit(solution)/shard_map/all_gather | solution.py:120
  9.7 106.5 %collective-permute-start = (bf16[1792,64]{0,1:T(8,128)(2,1)}, bf16[1792,64]{0,1:T(8,128)(2,1)}, u32[]{:S(2)}, u32[]{:S(2)}) collective-permute-start(bf16[1792,64]{0,1:T(8,128)(2,1)} %slice.43), channel_id=1, source_target_pairs={{0,8},{8,0},{16,24},{24,16},{32,40},{40,32},{48,56},{56,48},{64,72... | collective-permute-start | bytes 688136 | tf_op jit(solution)/shard_map/ppermute | solution.py:19
  11.3 103.0 %collective-permute-start.5 = (bf16[1792,64]{0,1:T(8,128)(2,1)}, bf16[1792,64]{0,1:T(8,128)(2,1)}, u32[]{:S(2)}, u32[]{:S(2)}) collective-permute-start(bf16[1792,64]{0,1:T(8,128)(2,1)} %slice.45), channel_id=1, source_target_pairs={{0,8},{8,0},{16,24},{24,16},{32,40},{40,32},{48,56},{56,48},{64,72... | collective-permute-start | bytes 688136 | tf_op jit(solution)/shard_map/ppermute | solution.py:19
  18.3 74.5 %copy-start.19 = (pred[512]{0:T(512)(128)(4,1)}, pred[512]{0:T(512)(128)(4,1)S(1)}, u32[]{:S(2)}) copy-start(pred[512]{0:T(512)(128)(4,1)S(1)} %compare_and_fusion.1) | copy-start | bytes 1540
  87.8 20.3 %copy-start.4 = (bf16[512,256]{1,0:T(8,128)(2,1)}, bf16[512,256]{1,0:T(8,128)(2,1)S(1)}, u32[]{:S(2)}) copy-start(bf16[512,256]{1,0:T(8,128)(2,1)S(1)} %gather_fusion) | copy-start | bytes 786436
  88.6 18.3 %collective-permute-start.1 = (bf16[512,256]{1,0:T(8,128)(2,1)}, bf16[512,256]{1,0:T(8,128)(2,1)}, u32[]{:S(2)}, u32[]{:S(2)}) collective-permute-start(bf16[512,256]{1,0:T(8,128)(2,1)} %broadcast_select_fusion.2), channel_id=1, source_target_pairs={{0,1},{1,0},{2,3},{3,2},{4,5},{5,4},{6,7},{7,6},{8,9},{9,8},{10,11... | collective-permute-start | bytes 786440 | tf_op jit(solution)/shard_map/ppermute | solution.py:19
  93.4 21.0 %copy-start.9 = (bf16[2048,64]{0,1:T(8,128)(2,1)S(1)}, bf16[2048,64]{0,1:T(8,128)(2,1)}, u32[]{:S(2)}) copy-start(bf16[2048,64]{0,1:T(8,128)(2,1)} %param.36) | copy-start | bytes 786436
  95.8 20.4 %copy-start.10 = (bf16[2048,64]{0,1:T(8,128)(2,1)S(1)}, bf16[2048,64]{0,1:T(8,128)(2,1)}, u32[]{:S(2)}) copy-start(bf16[2048,64]{0,1:T(8,128)(2,1)} %param.37) | copy-start | bytes 786436
  108.1 16.5 %collective-permute-start.3 = (bf16[2,512,256]{2,1,0:T(8,128)(2,1)S(1)}, bf16[2,512,256]{2,1,0:T(8,128)(2,1)S(1)}, u32[]{:S(2)}, u32[]{:S(2)}) collective-permute-start(bf16[2,512,256]{2,1,0:T(8,128)(2,1)S(1)} %get-tuple-element.34), channel_id=1, source_target_pairs={{0,4},{1,5},{2,6},{3,7},{4,0},{5,1},{6,2},{7,3},{8,12},{9,13},{10,... | collective-permute-start | bytes 1572872 | tf_op jit(solution)/shard_map/ppermute | solution.py:15
  111.2 23.0 %collective-permute-start.2 = (bf16[2,512,256]{2,1,0:T(8,128)(2,1)S(1)}, bf16[2,512,256]{2,1,0:T(8,128)(2,1)S(1)}, u32[]{:S(2)}, u32[]{:S(2)}) collective-permute-start(bf16[2,512,256]{2,1,0:T(8,128)(2,1)S(1)} %get-tuple-element.34), channel_id=1, source_target_pairs={{0,2},{1,3},{2,4},{3,5},{4,6},{5,7},{6,0},{7,1},{8,10},{9,11},{10,... | collective-permute-start | bytes 1572872 | tf_op jit(solution)/shard_map/ppermute | solution.py:15
  111.7 22.5 %collective-permute-start.4 = (bf16[2,512,256]{2,1,0:T(8,128)(2,1)S(1)}, bf16[2,512,256]{2,1,0:T(8,128)(2,1)S(1)}, u32[]{:S(2)}, u32[]{:S(2)}) collective-permute-start(bf16[2,512,256]{2,1,0:T(8,128)(2,1)S(1)} %get-tuple-element.34), channel_id=1, source_target_pairs={{0,6},{1,7},{2,0},{3,1},{4,2},{5,3},{6,4},{7,5},{8,14},{9,15},{10,... | collective-permute-start | bytes 1572872 | tf_op jit(solution)/shard_map/ppermute | solution.py:15
  149.8 8.0 %copy-start.16 = (f32[4,2,256]{2,1,0:T(2,128)S(1)}, f32[4,2,256]{2,1,0:T(2,128)}, u32[]{:S(2)}) copy-start(f32[4,2,256]{2,1,0:T(2,128)} %mul.193) | copy-start | bytes 24580
  191.6 15.6 %copy-start.3 = (f32[2,256,2048]{2,1,0:T(8,128)S(1)}, f32[2,256,2048]{2,1,0:T(8,128)}, u32[]{:S(2)}) copy-start(f32[2,256,2048]{2,1,0:T(8,128)} %reshape.510) | copy-start | bytes 12582916
  191.6 15.6 %copy-start.12 = (bf16[2048,64]{0,1:T(8,128)(2,1)S(1)}, bf16[2048,64]{0,1:T(8,128)(2,1)}, u32[]{:S(2)}) copy-start(bf16[2048,64]{0,1:T(8,128)(2,1)} %param.30) | copy-start | bytes 786436
  191.6 15.6 %copy-start.22 = (f32[2,256]{1,0:T(2,128)S(1)}, f32[2,256]{1,0:T(2,128)}, u32[]{:S(2)}) copy-start(f32[2,256]{1,0:T(2,128)} %rsqrt.21) | copy-start | bytes 6148
  208.1 16.0 %copy-start.8 = (bf16[256,2048]{1,0:T(8,128)(2,1)S(1)}, bf16[256,2048]{1,0:T(8,128)(2,1)}, u32[]{:S(2)}) copy-start(bf16[256,2048]{1,0:T(8,128)(2,1)} %param.31) | copy-start | bytes 3145732
  239.9 25.3 %collective-permute-start.8 = (bf16[512,512]{1,0:T(8,128)(2,1)S(1)}, bf16[512,512]{1,0:T(8,128)(2,1)}, u32[]{:S(2)}, u32[]{:S(2)}) collective-permute-start(bf16[512,512]{1,0:T(8,128)(2,1)S(1)} %fusion.47), channel_id=1, source_target_pairs={{0,6},{1,7},{2,0},{3,1},{4,2},{5,3},{6,4},{7,5},{8,14},{9,15},{10,... | collective-permute-start | bytes 1572872 | tf_op jit(solution)/shard_map/ppermute | solution.py:15
  243.5 26.3 %collective-permute-start.6 = (bf16[512,512]{1,0:T(8,128)(2,1)}, bf16[512,512]{1,0:T(8,128)(2,1)}, u32[]{:S(2)}, u32[]{:S(2)}) collective-permute-start(bf16[512,512]{1,0:T(8,128)(2,1)} %fusion.49), channel_id=1, source_target_pairs={{0,2},{1,3},{2,4},{3,5},{4,6},{5,7},{6,0},{7,1},{8,10},{9,11},{10,... | collective-permute-start | bytes 1572872 | tf_op jit(solution)/shard_map/ppermute | solution.py:15
  244.4 25.4 %collective-permute-start.7 = (bf16[512,512]{1,0:T(8,128)(2,1)}, bf16[512,512]{1,0:T(8,128)(2,1)}, u32[]{:S(2)}, u32[]{:S(2)}) collective-permute-start(bf16[512,512]{1,0:T(8,128)(2,1)} %fusion.48), channel_id=1, source_target_pairs={{0,4},{1,5},{2,6},{3,7},{4,0},{5,1},{6,2},{7,3},{8,12},{9,13},{10,... | collective-permute-start | bytes 1572872 | tf_op jit(solution)/shard_map/ppermute | solution.py:15
  277.7 18.5 %copy-start.20 = (pred[512]{0:T(512)(128)(4,1)S(1)}, pred[512]{0:T(512)(128)(4,1)}, u32[]{:S(2)}) copy-start(pred[512]{0:T(512)(128)(4,1)} %copy-done.19) | copy-start | bytes 1540
  282.1 14.1 %collective-permute-start.9 = (bf16[512,256]{1,0:T(8,128)(2,1)S(1)}, bf16[512,256]{1,0:T(8,128)(2,1)S(1)}, u32[]{:S(2)}, u32[]{:S(2)}) collective-permute-start(bf16[512,256]{1,0:T(8,128)(2,1)S(1)} %fusion.55), channel_id=1, source_target_pairs={{0,1},{1,0},{2,3},{3,2},{4,5},{5,4},{6,7},{7,6},{8,9},{9,8},{10,11... | collective-permute-start | bytes 786440 | tf_op jit(solution)/shard_map/ppermute | solution.py:19
  297.3 13.0 %copy-start.5 = (bf16[512,256]{1,0:T(8,128)(2,1)}, bf16[512,256]{1,0:T(8,128)(2,1)S(1)}, u32[]{:S(2)}) copy-start(bf16[512,256]{1,0:T(8,128)(2,1)S(1)} %fusion.54) | copy-start | bytes 786436
  297.3 13.0 %collective-permute-start.10 = (bf16[512,256]{1,0:T(8,128)(2,1)S(1)}, bf16[512,256]{1,0:T(8,128)(2,1)S(1)}, u32[]{:S(2)}, u32[]{:S(2)}) collective-permute-start(bf16[512,256]{1,0:T(8,128)(2,1)S(1)} %fusion.54), channel_id=1, source_target_pairs={{0,1},{1,0},{2,3},{3,2},{4,5},{5,4},{6,7},{7,6},{8,9},{9,8},{10,11... | collective-permute-start | bytes 786440 | tf_op jit(solution)/shard_map/ppermute | solution.py:19
  310.5 16.4 %collective-permute-start.12 = (bf16[2,512,256]{2,1,0:T(8,128)(2,1)S(1)}, bf16[2,512,256]{2,1,0:T(8,128)(2,1)S(1)}, u32[]{:S(2)}, u32[]{:S(2)}) collective-permute-start(bf16[2,512,256]{2,1,0:T(8,128)(2,1)S(1)} %get-tuple-element.30), channel_id=1, source_target_pairs={{0,4},{1,5},{2,6},{3,7},{4,0},{5,1},{6,2},{7,3},{8,12},{9,13},{10,... | collective-permute-start | bytes 1572872 | tf_op jit(solution)/shard_map/ppermute | solution.py:15
  311.4 25.6 %collective-permute-start.11 = (bf16[2,512,256]{2,1,0:T(8,128)(2,1)S(1)}, bf16[2,512,256]{2,1,0:T(8,128)(2,1)S(1)}, u32[]{:S(2)}, u32[]{:S(2)}) collective-permute-start(bf16[2,512,256]{2,1,0:T(8,128)(2,1)S(1)} %get-tuple-element.30), channel_id=1, source_target_pairs={{0,2},{1,3},{2,4},{3,5},{4,6},{5,7},{6,0},{7,1},{8,10},{9,11},{10,... | collective-permute-start | bytes 1572872 | tf_op jit(solution)/shard_map/ppermute | solution.py:15
  311.4 25.6 %collective-permute-start.13 = (bf16[2,512,256]{2,1,0:T(8,128)(2,1)S(1)}, bf16[2,512,256]{2,1,0:T(8,128)(2,1)S(1)}, u32[]{:S(2)}, u32[]{:S(2)}) collective-permute-start(bf16[2,512,256]{2,1,0:T(8,128)(2,1)S(1)} %get-tuple-element.30), channel_id=1, source_target_pairs={{0,6},{1,7},{2,0},{3,1},{4,2},{5,3},{6,4},{7,5},{8,14},{9,15},{10,... | collective-permute-start | bytes 1572872 | tf_op jit(solution)/shard_map/ppermute | solution.py:15
  379.9 14.9 %collective-permute-start.16 = (bf16[512,512]{1,0:T(8,128)(2,1)S(1)}, bf16[512,512]{1,0:T(8,128)(2,1)S(1)}, u32[]{:S(2)}, u32[]{:S(2)}) collective-permute-start(bf16[512,512]{1,0:T(8,128)(2,1)S(1)} %fusion.43), channel_id=1, source_target_pairs={{0,6},{1,7},{2,0},{3,1},{4,2},{5,3},{6,4},{7,5},{8,14},{9,15},{10,... | collective-permute-start | bytes 1572872 | tf_op jit(solution)/shard_map/ppermute | solution.py:15
  380.5 25.8 %collective-permute-start.14 = (bf16[512,512]{1,0:T(8,128)(2,1)S(1)}, bf16[512,512]{1,0:T(8,128)(2,1)S(1)}, u32[]{:S(2)}, u32[]{:S(2)}) collective-permute-start(bf16[512,512]{1,0:T(8,128)(2,1)S(1)} %fusion.45), channel_id=1, source_target_pairs={{0,2},{1,3},{2,4},{3,5},{4,6},{5,7},{6,0},{7,1},{8,10},{9,11},{10,... | collective-permute-start | bytes 1572872 | tf_op jit(solution)/shard_map/ppermute | solution.py:15
  382.0 24.4 %collective-permute-start.15 = (bf16[512,512]{1,0:T(8,128)(2,1)S(1)}, bf16[512,512]{1,0:T(8,128)(2,1)S(1)}, u32[]{:S(2)}, u32[]{:S(2)}) collective-permute-start(bf16[512,512]{1,0:T(8,128)(2,1)S(1)} %fusion.44), channel_id=1, source_target_pairs={{0,4},{1,5},{2,6},{3,7},{4,0},{5,1},{6,2},{7,3},{8,12},{9,13},{10,... | collective-permute-start | bytes 1572872 | tf_op jit(solution)/shard_map/ppermute | solution.py:15
  416.8 10.4 %collective-permute-start.17 = (bf16[512,256]{1,0:T(8,128)(2,1)S(1)}, bf16[512,256]{1,0:T(8,128)(2,1)S(1)}, u32[]{:S(2)}, u32[]{:S(2)}) collective-permute-start(bf16[512,256]{1,0:T(8,128)(2,1)S(1)} %fusion.56), channel_id=1, source_target_pairs={{0,1},{1,0},{2,3},{3,2},{4,5},{5,4},{6,7},{7,6},{8,9},{9,8},{10,11... | collective-permute-start | bytes 786440 | tf_op jit(solution)/shard_map/ppermute | solution.py:19
  (12 other events, 34.6 us)
Sparse Core Ops, SparseCore 0:
  9.9 71.8 all-gather.1

commit v2 on v1

--- a/solution.py
+++ b/solution.py
@@ -2,6 +2,8 @@
 import jax.numpy as jnp
 from jax import lax
 from jax.sharding import PartitionSpec as P
+from jax.experimental import pallas as pl
+from jax.experimental.pallas import tpu as pltpu
 
 HD = 64
 
@@ -26,12 +28,17 @@
     mine_x = me // 2
     partner = swapped(part, "tp", 0)
     low_first = me % 2 == 0
-    pair = jnp.stack([jnp.where(low_first, part, partner), jnp.where(low_first, partner, part)])
-    received = [pair] + [shifted(pair, "tp", 2 * k) for k in range(1, n_x)]
-    stacked = jnp.stack(received)
-    order = (mine_x - jnp.arange(n_x, dtype=jnp.int32)) % n_x
-    full = jnp.take(stacked, order, axis=0)
-    return full.transpose(2, 0, 1, 3).reshape(rows, n_x * 2 * width)
+    pair = jnp.where(
+        low_first,
+        jnp.concatenate([part, partner], axis=1),
+        jnp.concatenate([partner, part], axis=1),
+    )
+    full = jnp.zeros((rows, n_x * 2 * width), part.dtype)
+    full = lax.dynamic_update_slice(full, pair, (0, mine_x * 2 * width))
+    for k in range(1, n_x):
+        got = shifted(pair, "tp", 2 * k)
+        full = lax.dynamic_update_slice(full, got, (0, ((mine_x - k) % n_x) * 2 * width))
+    return full
 
 
 def tp_reduce(full):
@@ -39,10 +46,10 @@
     n_x = lax.axis_size("tp") // 2
     me = lax.axis_index("tp")
     mine_x = me // 2
-    pieces = full.reshape(rows, n_x, total_width // n_x)
-    acc = jnp.take(pieces, mine_x, axis=1).astype(jnp.float32)
+    span = total_width // n_x
+    acc = lax.dynamic_slice_in_dim(full, mine_x * span, span, 1).astype(jnp.float32)
     for k in range(1, n_x):
-        piece = jnp.take(pieces, (mine_x + k) % n_x, axis=1)
+        piece = lax.dynamic_slice_in_dim(full, ((mine_x + k) % n_x) * span, span, 1)
         acc = acc + shifted(piece, "tp", 2 * k).astype(jnp.float32)
     halves = acc.reshape(rows, 2, total_width // n_x // 2)
     low = me % 2 == 0
@@ -71,16 +78,62 @@
     )
 
 
-def partial_attention(query, keys, values, valid):
-    scores = jnp.einsum("pbcgd,pkcd->pbcgk", query, keys, preferred_element_type=jnp.float32) * 0.125
-    scores = jnp.where(valid, scores, SENTINEL)
-    top = jnp.max(scores, axis=-1)
-    weights = jnp.where(valid, jnp.exp(scores - top[..., None]), 0.0)
-    total = jnp.sum(weights, axis=-1)
-    weighted = jnp.einsum(
-        "pbcgk,pkcd->pbcgd", weights.astype(jnp.bfloat16), values, preferred_element_type=jnp.float32
-    )
-    return (weighted, top, total)
+def attention_kernel(q_ref, ko_ref, kf_ref, kn_ref, vo_ref, vf_ref, vn_ref, mo_ref, mf_ref, o_ref):
+    query = q_ref[0]
+    contract = (((1,), (1,)), ((), ()))
+    parts = []
+    for keys, mask in ((ko_ref[...], mo_ref[...]), (kf_ref[...], mf_ref[...]), (kn_ref[0], None)):
+        scores = lax.dot_general(query, keys, contract, preferred_element_type=jnp.float32) * 0.125
+        if mask is not None:
+            scores = jnp.where(mask > 0, scores, SENTINEL)
+        parts.append((scores, mask))
+    top = parts[0][0].max(axis=-1, keepdims=True)
+    for scores, _ in parts[1:]:
+        top = jnp.maximum(top, scores.max(axis=-1, keepdims=True))
+    total = jnp.zeros_like(top)
+    weighted = jnp.zeros((query.shape[0], vn_ref.shape[-1]), jnp.float32)
+    for (scores, mask), values in zip(parts, (vo_ref[...], vf_ref[...], vn_ref[0])):
+        weights = jnp.exp(scores - top)
+        if mask is not None:
+            weights = jnp.where(mask > 0, weights, 0.0)
+        total = total + weights.sum(axis=-1, keepdims=True)
+        weighted = weighted + jnp.dot(
+            weights.astype(jnp.bfloat16), values, preferred_element_type=jnp.float32
+        )
+    o_ref[0] = (weighted / total).astype(o_ref.dtype)
+
+
+def attention(query, own_keys, far_keys, new_keys, own_values, far_values, new_values, own_mask, far_mask):
+    passes, rows, depth = query.shape
+    tile = 256
+    n_own = own_keys.shape[0]
+    n_far = far_keys.shape[0]
+    n_new = new_keys.shape[1]
+    n_keys = n_own + n_far + n_new
+    whole = lambda shape: pl.BlockSpec(shape, lambda p, i: (0,) * len(shape))
+    per_pass = pl.BlockSpec((1, n_new, depth), lambda p, i: (p, 0, 0))
+    return pl.pallas_call(
+        attention_kernel,
+        grid=(passes, rows // tile),
+        in_specs=[
+            pl.BlockSpec((1, tile, depth), lambda p, i: (p, i, 0)),
+            whole((n_own, depth)),
+            whole((n_far, depth)),
+            per_pass,
+            whole((n_own, depth)),
+            whole((n_far, depth)),
+            per_pass,
+            whole((1, n_own)),
+            whole((1, n_far)),
+        ],
+        out_specs=pl.BlockSpec((1, tile, depth), lambda p, i: (p, i, 0)),
+        out_shape=jax.ShapeDtypeStruct(query.shape, jnp.bfloat16),
+        cost_estimate=pl.CostEstimate(
+            flops=4 * passes * rows * n_keys * depth,
+            transcendentals=passes * rows * n_keys,
+            bytes_accessed=2 * (2 * passes * rows * depth + 2 * n_keys * depth),
+        ),
+    )(query, own_keys, far_keys, new_keys, own_values, far_values, new_values, own_mask, far_mask)
 
 
 def on_device(
@@ -127,7 +180,6 @@
     far_values = tail_values.reshape(slots - block, stored_local, HD)
     far_valid = tail_ids >= slots - far_count
     own_valid = slot_ids < own_count
-    valid = jnp.concatenate([own_valid, far_valid, jnp.ones((block,), dtype=bool)])
 
     x_full = tp_gather(x_part)
     normed = rms_normed(x_full.astype(jnp.float32), attn_gain)
@@ -150,17 +202,18 @@
         .reshape(2, block, stored_local, HD)
         .astype(jnp.bfloat16)
     )
-    cached_keys = jnp.concatenate([store_keys, far_keys], axis=0)
-    cached_values = jnp.concatenate([store_values, far_values], axis=0)
-    keys = jnp.concatenate(
-        [jnp.broadcast_to(cached_keys[None], (2,) + cached_keys.shape), new_keys], axis=1
-    )
-    values = jnp.concatenate(
-        [jnp.broadcast_to(cached_values[None], (2,) + cached_values.shape), new_values], axis=1
-    )
-    weighted, top, total = partial_attention(query, keys, values, valid)
-    attended = weighted / total[..., None]
-    mixed = attended.reshape(rows, query_local * HD).astype(jnp.bfloat16)
+    mixed_heads = attention(
+        query.reshape(2, block * per_stored, HD),
+        store_keys.reshape(slots, HD),
+        far_keys.reshape(slots - block, HD),
+        new_keys.reshape(2, block, HD),
+        store_values.reshape(slots, HD),
+        far_values.reshape(slots - block, HD),
+        new_values.reshape(2, block, HD),
+        own_valid.astype(jnp.int32)[None],
+        far_valid.astype(jnp.int32)[None],
+    )
+    mixed = mixed_heads.reshape(rows, query_local * HD)
     head_term = jnp.dot(mixed, w_out, preferred_element_type=jnp.float32)
     head_sum = tp_reduce(head_term.astype(jnp.bfloat16))
     resid_part = (x_part.astype(jnp.float32) + head_sum).astype(jnp.bfloat16)

time: 444 us -> 350 us (0.79)
  the two profiles are of different devices: /device:TPU:32 before, /device:TPU:72 now
where the time goes in v2:
time: 350 us; the launch traced here: 347 us
  waiting for transfers between devices  192 us (55%)
  local copies, waits for them, and re-layouts  47.7 us (14%)
  starting transfers between devices  31.8 us (9%)
  Pallas kernels  20.6 us (6%)
  other arithmetic  19.3 us (6%)
  matrix products  19 us (5%)
  between operations  16.3 us (5%)
    ppermute x12, waiting for transfers between devices, shifted(): return lax.ppermute(array, axis, [(i, (i + step) % n) for i in range(n)])  83.5 us
    all_gather x1, waiting for transfers between devices, on_device(): table = lax.all_gather(embed, 'grp', axis=0, tiled=True)  64.6 us
    ppermute x6, waiting for transfers between devices, swapped(): lax.ppermute(array, axis, [(i, i ^ 1 << bit) for i in range(lax.axis_size...  43.5 us
    pallas_call x1, Pallas kernels, attention(): pl.pallas_call(attention_kernel, grid=(passes, rows // tile), in_specs=[p...  20.6 us
    ppermute x12, starting transfers between devices, shifted(): return lax.ppermute(array, axis, [(i, (i + step) % n) for i in range(n)])  18.4 us
    ppermute x6, starting transfers between devices, swapped(): lax.ppermute(array, axis, [(i, i ^ 1 << bit) for i in range(lax.axis_size...  13.4 us
    unnamed x32, local copies, waits for them, and re-layouts  10.1 us
    dot_general x1, matrix products, on_device(): down_term = jnp.dot(hidden, w_down, preferred_element_type=jnp.float32)  7.77 us
  transfers between devices with their start and end apart: 19, of which 13 were waited for; matrix products, arithmetic and copies ran while one was open for 15% of the time, Pallas kernels for 0%

profile of v2, /device:TPU:72, one launch (start us, length us, event | category | flops | bytes accessed | tf_op | source)
XLA Modules:
  0.0 347.1 jit_solution(12009364411138206759)
XLA Ops:
  15.9 64.6 %all-gather.2.cloned.1.call-done = bf16[16384,256]{1,0:T(8,128)(2,1)} async-done(((bf16[512,256]{1,0:T(8,128)(2,1)}), bf16[16384,256]{1,0:T(8,128)(2,1)}) %all-gather.2.cloned.1.call-update) | async-done | bytes 8388624 | tf_op jit(solution)/shard_map/all_gather | solution.py:173
  80.5 6.0 %gather_fusion = bf16[512,256]{1,0:T(8,128)(2,1)S(1)} fusion(bf16[16384,256]{1,0:T(8,128)(2,1)} %all-gather.2.cloned.1.call-done, s32[1024]{0:T(1024)S(1)} %pad_clamp_fusion), kind=kCustom, calls=%fused_computation | custom fusion | bytes 526336 | tf_op jit(solution)/shard_map/jit(_take)/gather | solution.py:175
  86.7 3.6 %collective-permute-start = (bf16[512,256]{1,0:T(8,128)(2,1)S(1)}, bf16[512,256]{1,0:T(8,128)(2,1)}, u32[]{:S(2)}, u32[]{:S(2)}) collective-permute-start(bf16[512,256]{1,0:T(8,128)(2,1)S(1)} %broadcast_select_fusion), channel_id=1, source_target_pairs={{0,1},{1,0},{2,3},{3,2},{4,5},{5,4},{6,7},{7,6},{8,9},{9,8},{10,11... | collective-permute-start | bytes 786440 | tf_op jit(solution)/shard_map/ppermute | solution.py:21
  92.8 12.0 %collective-permute-done = bf16[512,256]{1,0:T(8,128)(2,1)} collective-permute-done((bf16[512,256]{1,0:T(8,128)(2,1)S(1)}, bf16[512,256]{1,0:T(8,128)(2,1)}, u32[]{:S(2)}, u32[]{:S(2)}) %collective-permute-start) | collective-permute-done | bytes 262176 | tf_op jit(solution)/shard_map/ppermute | solution.py:21
  110.7 2.8 collective-permute-start.2
  117.3 6.7 %collective-permute-done.1 = bf16[512,512]{1,0:T(8,128)(2,1)} collective-permute-done((bf16[512,512]{1,0:T(8,128)(2,1)}, bf16[512,512]{1,0:T(8,128)(2,1)}, u32[]{:S(2)}, u32[]{:S(2)}) %collective-permute-start.1) | collective-permute-done | bytes 524320 | tf_op jit(solution)/shard_map/ppermute | solution.py:17
  126.0 9.5 %collective-permute-done.2 = bf16[512,512]{1,0:T(8,128)(2,1)} collective-permute-done((bf16[512,512]{1,0:T(8,128)(2,1)}, bf16[512,512]{1,0:T(8,128)(2,1)}, u32[]{:S(2)}, u32[]{:S(2)}) %collective-permute-start.2) | collective-permute-done | bytes 524320 | tf_op jit(solution)/shard_map/ppermute | solution.py:17
  149.1 2.6 fusion.33
  154.8 2.3 copy.46
  157.1 3.0 convolution_convert_fusion.2
  165.8 20.6 %shard_map.176 = bf16[2,1024,64]{2,1,0:T(8,128)(2,1)} custom-call(bf16[2,1024,64]{2,1,0:T(8,128)(2,1)} %pad_maximum_fusion.q_ref, bf16[2048,64]{1,0:T(8,128)(2,1)} %copy-done.3, bf16[1792,64]{1,0:T(8,128)(2,1)} %collective-permute-done.4.kf_ref, bf16[2,256,64]{2,1,0:T(8,128)(2,1)} %pad_maximum_fusion.1.kn_ref, bf16[2048,64]{1,0:T(8,128)(2,1)} %copy.40.vo_ref, ...), custom_call_target="tpu_custom_call" | custom-call | flops 2147483648 | bytes 1572864 | tf_op jit(solution)/shard_map/pallas_call | solution.py:115
  190.3 2.4 collective-permute-start.7
  194.2 9.4 %collective-permute-done.6 = bf16[512,512]{1,0:T(8,128)(2,1)S(1)} collective-permute-done((bf16[512,512]{1,0:T(8,128)(2,1)S(1)}, bf16[512,512]{1,0:T(8,128)(2,1)S(1)}, u32[]{:S(2)}, u32[]{:S(2)}) %collective-permute-start.6) | collective-permute-done | bytes 524320 | tf_op jit(solution)/shard_map/ppermute | solution.py:17
  203.6 12.1 %collective-permute-done.7 = bf16[512,512]{1,0:T(8,128)(2,1)S(1)} collective-permute-done((bf16[512,512]{1,0:T(8,128)(2,1)S(1)}, bf16[512,512]{1,0:T(8,128)(2,1)S(1)}, u32[]{:S(2)}, u32[]{:S(2)}) %collective-permute-start.7) | collective-permute-done | bytes 524320 | tf_op jit(solution)/shard_map/ppermute | solution.py:17
  217.0 2.8 reshape.287
  219.9 2.5 fusion.30
  222.4 3.6 %collective-permute-start.9 = (bf16[512,256]{1,0:T(8,128)(2,1)S(1)}, bf16[512,256]{1,0:T(8,128)(2,1)S(1)}, u32[]{:S(2)}, u32[]{:S(2)}) collective-permute-start(bf16[512,256]{1,0:T(8,128)(2,1)S(1)} %fusion.17), channel_id=1, source_target_pairs={{0,1},{1,0},{2,3},{3,2},{4,5},{5,4},{6,7},{7,6},{8,9},{9,8},{10,11... | collective-permute-start | bytes 786440 | tf_op jit(solution)/shard_map/ppermute | solution.py:21
  226.0 10.7 %collective-permute-done.9 = bf16[512,256]{1,0:T(8,128)(2,1)S(1)} collective-permute-done((bf16[512,256]{1,0:T(8,128)(2,1)S(1)}, bf16[512,256]{1,0:T(8,128)(2,1)S(1)}, u32[]{:S(2)}, u32[]{:S(2)}) %collective-permute-start.9) | collective-permute-done | bytes 262176 | tf_op jit(solution)/shard_map/ppermute | solution.py:21
  236.9 4.8 %collective-permute-start.10 = (bf16[512,256]{1,0:T(8,128)(2,1)S(1)}, bf16[512,256]{1,0:T(8,128)(2,1)S(1)}, u32[]{:S(2)}, u32[]{:S(2)}) collective-permute-start(bf16[512,256]{1,0:T(8,128)(2,1)S(1)} %fusion.16), channel_id=1, source_target_pairs={{0,1},{1,0},{2,3},{3,2},{4,5},{5,4},{6,7},{7,6},{8,9},{9,8},{10,11... | collective-permute-start | bytes 786440 | tf_op jit(solution)/shard_map/ppermute | solution.py:21
  241.6 10.3 %collective-permute-done.10 = bf16[512,256]{1,0:T(8,128)(2,1)S(1)} collective-permute-done((bf16[512,256]{1,0:T(8,128)(2,1)S(1)}, bf16[512,256]{1,0:T(8,128)(2,1)S(1)}, u32[]{:S(2)}, u32[]{:S(2)}) %collective-permute-start.10) | collective-permute-done | bytes 262176 | tf_op jit(solution)/shard_map/ppermute | solution.py:21
  253.9 3.0 collective-permute-start.12
  256.9 10.6 %collective-permute-done.11 = bf16[512,512]{1,0:T(8,128)(2,1)S(1)} collective-permute-done((bf16[512,512]{1,0:T(8,128)(2,1)S(1)}, bf16[512,512]{1,0:T(8,128)(2,1)S(1)}, u32[]{:S(2)}, u32[]{:S(2)}) %collective-permute-start.11) | collective-permute-done | bytes 524320 | tf_op jit(solution)/shard_map/ppermute | solution.py:17
  267.7 12.3 %collective-permute-done.12 = bf16[512,512]{1,0:T(8,128)(2,1)S(1)} collective-permute-done((bf16[512,512]{1,0:T(8,128)(2,1)S(1)}, bf16[512,512]{1,0:T(8,128)(2,1)S(1)}, u32[]{:S(2)}, u32[]{:S(2)}) %collective-permute-start.12) | collective-permute-done | bytes 524320 | tf_op jit(solution)/shard_map/ppermute | solution.py:17
  281.5 2.9 fusion.11
  284.4 7.8 %convolution_convert_fusion.1 = bf16[512,2048]{1,0:T(8,128)(2,1)} fusion(bf16[704,2048]{1,0:T(8,128)(2,1)S(1)} %copy-done, f32[512,704]{0,1:T(8,128)} %fusion.11, bf16[2048,704]{0,1:T(8,128)(2,1)} %param.30, bf16[512,2048]{1,0:T(8,128)(2,1)} %copy-done.2, f32[2048]{0:T(1024)S(1)} %copy-done.11, f32[512]{0:T(512)S(1)} %add_rsqrt_fusion), kind=kOutput, calls=%fused_computation.12 | convolution fusion | flops 2960195584 | bytes 11413504 | tf_op jit(solution)/shard_map/dot_general | solution.py:225
  294.3 3.0 collective-permute-start.15
  297.5 10.4 %collective-permute-done.14 = bf16[512,512]{1,0:T(8,128)(2,1)S(1)} collective-permute-done((bf16[512,512]{1,0:T(8,128)(2,1)S(1)}, bf16[512,512]{1,0:T(8,128)(2,1)S(1)}, u32[]{:S(2)}, u32[]{:S(2)}) %collective-permute-start.14) | collective-permute-done | bytes 524320 | tf_op jit(solution)/shard_map/ppermute | solution.py:17
  307.9 12.4 %collective-permute-done.15 = bf16[512,512]{1,0:T(8,128)(2,1)S(1)} collective-permute-done((bf16[512,512]{1,0:T(8,128)(2,1)S(1)}, bf16[512,512]{1,0:T(8,128)(2,1)S(1)}, u32[]{:S(2)}, u32[]{:S(2)}) %collective-permute-start.15) | collective-permute-done | bytes 524320 | tf_op jit(solution)/shard_map/ppermute | solution.py:17
  320.3 2.3 convert_add_fusion
  322.6 2.9 reshape.288
  325.5 2.5 fusion.29
  328.9 10.5 %collective-permute-done.17 = bf16[512,256]{1,0:T(8,128)(2,1)S(1)} collective-permute-done((bf16[512,256]{1,0:T(8,128)(2,1)S(1)}, bf16[512,256]{1,0:T(8,128)(2,1)S(1)}, u32[]{:S(2)}, u32[]{:S(2)}) %collective-permute-start.17) | collective-permute-done | bytes 262176 | tf_op jit(solution)/shard_map/ppermute | solution.py:21
  (100 shorter events, 57.8 us)
Async XLA Ops:
  7.2 277.2 %copy-start = (bf16[704,2048]{1,0:T(8,128)(2,1)S(1)}, bf16[704,2048]{1,0:T(8,128)(2,1)}, u32[]{:S(2)}) copy-start(bf16[704,2048]{1,0:T(8,128)(2,1)} %param.31) | copy-start | bytes 8650756
  7.2 7.3 %copy-start.12 = (s32[32]{0:T(128)S(1)}, s32[32]{0:T(128)}, u32[]{:S(2)}) copy-start(s32[32]{0:T(128)} %param.21) | copy-start | bytes 388
  7.2 8.6 %copy-start.6 = (s32[256]{0:T(256)S(1)}, s32[256]{0:T(256)}, u32[]{:S(2)}) copy-start(s32[256]{0:T(256)} %param.17) | copy-start | bytes 3076
  7.2 8.6 %copy-start.9 = (s32[256]{0:T(256)S(1)}, s32[256]{0:T(256)}, u32[]{:S(2)}) copy-start(s32[256]{0:T(256)} %param.18) | copy-start | bytes 3076
  7.2 8.6 %copy-start.8 = (s32[256]{0:T(256)S(1)}, s32[256]{0:T(256)}, u32[]{:S(2)}) copy-start(s32[256]{0:T(256)} %param.19) | copy-start | bytes 3076
  7.2 73.3 %all-gather.2.cloned.1.call-start = ((), (), s32[]{:S(2)}) async-start(), calls=%async_computation | async-start | bytes 8650752 | tf_op jit(solution)/shard_map/all_gather | solution.py:173
  9.3 6.5 %copy-start.3 = (bf16[2048,64]{1,0:T(8,128)(2,1)}, bf16[2048,64]{1,0:T(8,128)(2,1)S(1)}, u32[]{:S(2)}) copy-start(bf16[2048,64]{1,0:T(8,128)(2,1)S(1)} %copy.39.ko_ref) | copy-start | bytes 786436
  10.2 155.5 %collective-permute-start.4 = (bf16[1792,64]{1,0:T(8,128)(2,1)}, bf16[1792,64]{1,0:T(8,128)(2,1)}, u32[]{:S(2)}, u32[]{:S(2)}) collective-permute-start(bf16[1792,64]{1,0:T(8,128)(2,1)} %slice.60), channel_id=1, source_target_pairs={{0,8},{8,0},{16,24},{24,16},{32,40},{40,32},{48,56},{56,48},{64,72... | collective-permute-start | bytes 688136 | tf_op jit(solution)/shard_map/ppermute | solution.py:21
  12.2 78.1 %copy-start.13 = (s32[32]{0:T(128)S(1)}, s32[32]{0:T(128)}, u32[]{:S(2)}) copy-start(s32[32]{0:T(128)} %param.20) | copy-start | bytes 388
  14.0 151.7 %collective-permute-start.5 = (bf16[1792,64]{1,0:T(8,128)(2,1)}, bf16[1792,64]{1,0:T(8,128)(2,1)}, u32[]{:S(2)}, u32[]{:S(2)}) collective-permute-start(bf16[1792,64]{1,0:T(8,128)(2,1)} %slice.63), channel_id=1, source_target_pairs={{0,8},{8,0},{16,24},{24,16},{32,40},{40,32},{48,56},{56,48},{64,72... | collective-permute-start | bytes 688136 | tf_op jit(solution)/shard_map/ppermute | solution.py:21
  86.7 18.2 %collective-permute-start = (bf16[512,256]{1,0:T(8,128)(2,1)S(1)}, bf16[512,256]{1,0:T(8,128)(2,1)}, u32[]{:S(2)}, u32[]{:S(2)}) collective-permute-start(bf16[512,256]{1,0:T(8,128)(2,1)S(1)} %broadcast_select_fusion), channel_id=1, source_target_pairs={{0,1},{1,0},{2,3},{3,2},{4,5},{5,4},{6,7},{7,6},{8,9},{9,8},{10,11... | collective-permute-start | bytes 786440 | tf_op jit(solution)/shard_map/ppermute | solution.py:21
  108.6 15.5 %collective-permute-start.1 = (bf16[512,512]{1,0:T(8,128)(2,1)}, bf16[512,512]{1,0:T(8,128)(2,1)}, u32[]{:S(2)}, u32[]{:S(2)}) collective-permute-start(bf16[512,512]{1,0:T(8,128)(2,1)} %get-tuple-element.5), channel_id=1, source_target_pairs={{0,2},{1,3},{2,4},{3,5},{4,6},{5,7},{6,0},{7,1},{8,10},{9,11},{10,... | collective-permute-start | bytes 1572872 | tf_op jit(solution)/shard_map/ppermute | solution.py:17
  110.7 24.8 %collective-permute-start.2 = (bf16[512,512]{1,0:T(8,128)(2,1)}, bf16[512,512]{1,0:T(8,128)(2,1)}, u32[]{:S(2)}, u32[]{:S(2)}) collective-permute-start(bf16[512,512]{1,0:T(8,128)(2,1)} %get-tuple-element.5), channel_id=1, source_target_pairs={{0,4},{1,5},{2,6},{3,7},{4,0},{5,1},{6,2},{7,3},{8,12},{9,13},{10,... | collective-permute-start | bytes 1572872 | tf_op jit(solution)/shard_map/ppermute | solution.py:17
  113.5 24.0 %collective-permute-start.3 = (bf16[512,512]{1,0:T(8,128)(2,1)}, bf16[512,512]{1,0:T(8,128)(2,1)}, u32[]{:S(2)}, u32[]{:S(2)}) collective-permute-start(bf16[512,512]{1,0:T(8,128)(2,1)} %get-tuple-element.5), channel_id=1, source_target_pairs={{0,6},{1,7},{2,0},{3,1},{4,2},{5,3},{6,4},{7,5},{8,14},{9,15},{10,... | collective-permute-start | bytes 1572872 | tf_op jit(solution)/shard_map/ppermute | solution.py:17
  126.0 15.4 %copy-start.7 = (f32[2048]{0:T(1024)S(1)}, f32[2048]{0:T(1024)}, u32[]{:S(2)}) copy-start(f32[2048]{0:T(1024)} %param.23) | copy-start | bytes 24580
  141.5 3.6 %copy-start.5 = (bf16[2048,64]{0,1:T(8,128)(2,1)S(1)}, bf16[2048,64]{0,1:T(8,128)(2,1)}, u32[]{:S(2)}) copy-start(bf16[2048,64]{0,1:T(8,128)(2,1)} %param.25) | copy-start | bytes 786436
  143.7 1.4 copy-start.1
  161.7 2.2 copy-start.4
  190.0 13.6 %collective-permute-start.6 = (bf16[512,512]{1,0:T(8,128)(2,1)S(1)}, bf16[512,512]{1,0:T(8,128)(2,1)S(1)}, u32[]{:S(2)}, u32[]{:S(2)}) collective-permute-start(bf16[512,512]{1,0:T(8,128)(2,1)S(1)} %get-tuple-element.11), channel_id=1, source_target_pairs={{0,2},{1,3},{2,4},{3,5},{4,6},{5,7},{6,0},{7,1},{8,10},{9,11},{10,... | collective-permute-start | bytes 1572872 | tf_op jit(solution)/shard_map/ppermute | solution.py:17
  190.3 25.4 %collective-permute-start.7 = (bf16[512,512]{1,0:T(8,128)(2,1)S(1)}, bf16[512,512]{1,0:T(8,128)(2,1)S(1)}, u32[]{:S(2)}, u32[]{:S(2)}) collective-permute-start(bf16[512,512]{1,0:T(8,128)(2,1)S(1)} %get-tuple-element.13), channel_id=1, source_target_pairs={{0,4},{1,5},{2,6},{3,7},{4,0},{5,1},{6,2},{7,3},{8,12},{9,13},{10,... | collective-permute-start | bytes 1572872 | tf_op jit(solution)/shard_map/ppermute | solution.py:17
  192.7 23.1 %collective-permute-start.8 = (bf16[512,512]{1,0:T(8,128)(2,1)S(1)}, bf16[512,512]{1,0:T(8,128)(2,1)S(1)}, u32[]{:S(2)}, u32[]{:S(2)}) collective-permute-start(bf16[512,512]{1,0:T(8,128)(2,1)S(1)} %get-tuple-element.12), channel_id=1, source_target_pairs={{0,6},{1,7},{2,0},{3,1},{4,2},{5,3},{6,4},{7,5},{8,14},{9,15},{10,... | collective-permute-start | bytes 1572872 | tf_op jit(solution)/shard_map/ppermute | solution.py:17
  222.4 14.3 %collective-permute-start.9 = (bf16[512,256]{1,0:T(8,128)(2,1)S(1)}, bf16[512,256]{1,0:T(8,128)(2,1)S(1)}, u32[]{:S(2)}, u32[]{:S(2)}) collective-permute-start(bf16[512,256]{1,0:T(8,128)(2,1)S(1)} %fusion.17), channel_id=1, source_target_pairs={{0,1},{1,0},{2,3},{3,2},{4,5},{5,4},{6,7},{7,6},{8,9},{9,8},{10,11... | collective-permute-start | bytes 786440 | tf_op jit(solution)/shard_map/ppermute | solution.py:21
  236.9 15.1 %collective-permute-start.10 = (bf16[512,256]{1,0:T(8,128)(2,1)S(1)}, bf16[512,256]{1,0:T(8,128)(2,1)S(1)}, u32[]{:S(2)}, u32[]{:S(2)}) collective-permute-start(bf16[512,256]{1,0:T(8,128)(2,1)S(1)} %fusion.16), channel_id=1, source_target_pairs={{0,1},{1,0},{2,3},{3,2},{4,5},{5,4},{6,7},{7,6},{8,9},{9,8},{10,11... | collective-permute-start | bytes 786440 | tf_op jit(solution)/shard_map/ppermute | solution.py:21
  252.4 15.2 %collective-permute-start.11 = (bf16[512,512]{1,0:T(8,128)(2,1)S(1)}, bf16[512,512]{1,0:T(8,128)(2,1)S(1)}, u32[]{:S(2)}, u32[]{:S(2)}) collective-permute-start(bf16[512,512]{1,0:T(8,128)(2,1)S(1)} %get-tuple-element.3), channel_id=1, source_target_pairs={{0,2},{1,3},{2,4},{3,5},{4,6},{5,7},{6,0},{7,1},{8,10},{9,11},{10,... | collective-permute-start | bytes 1572872 | tf_op jit(solution)/shard_map/ppermute | solution.py:17
  253.9 26.1 %collective-permute-start.12 = (bf16[512,512]{1,0:T(8,128)(2,1)S(1)}, bf16[512,512]{1,0:T(8,128)(2,1)S(1)}, u32[]{:S(2)}, u32[]{:S(2)}) collective-permute-start(bf16[512,512]{1,0:T(8,128)(2,1)S(1)} %get-tuple-element.3), channel_id=1, source_target_pairs={{0,4},{1,5},{2,6},{3,7},{4,0},{5,1},{6,2},{7,3},{8,12},{9,13},{10,... | collective-permute-start | bytes 1572872 | tf_op jit(solution)/shard_map/ppermute | solution.py:17
  256.9 23.1 %collective-permute-start.13 = (bf16[512,512]{1,0:T(8,128)(2,1)S(1)}, bf16[512,512]{1,0:T(8,128)(2,1)S(1)}, u32[]{:S(2)}, u32[]{:S(2)}) collective-permute-start(bf16[512,512]{1,0:T(8,128)(2,1)S(1)} %get-tuple-element.3), channel_id=1, source_target_pairs={{0,6},{1,7},{2,0},{3,1},{4,2},{5,3},{6,4},{7,5},{8,14},{9,15},{10,... | collective-permute-start | bytes 1572872 | tf_op jit(solution)/shard_map/ppermute | solution.py:17
  267.6 13.8 %copy-start.10 = (bf16[2048,704]{0,1:T(8,128)(2,1)S(1)}, bf16[2048,704]{0,1:T(8,128)(2,1)}, u32[]{:S(2)}) copy-start(bf16[2048,704]{0,1:T(8,128)(2,1)} %param.29) | copy-start | bytes 8650756
  267.7 13.8 %copy-start.11 = (f32[2048]{0:T(1024)S(1)}, f32[2048]{0:T(1024)}, u32[]{:S(2)}) copy-start(f32[2048]{0:T(1024)} %param.28) | copy-start | bytes 24580
  293.7 14.3 %collective-permute-start.14 = (bf16[512,512]{1,0:T(8,128)(2,1)S(1)}, bf16[512,512]{1,0:T(8,128)(2,1)S(1)}, u32[]{:S(2)}, u32[]{:S(2)}) collective-permute-start(bf16[512,512]{1,0:T(8,128)(2,1)S(1)} %get-tuple-element.8), channel_id=1, source_target_pairs={{0,2},{1,3},{2,4},{3,5},{4,6},{5,7},{6,0},{7,1},{8,10},{9,11},{10,... | collective-permute-start | bytes 1572872 | tf_op jit(solution)/shard_map/ppermute | solution.py:17
  294.3 26.1 %collective-permute-start.15 = (bf16[512,512]{1,0:T(8,128)(2,1)S(1)}, bf16[512,512]{1,0:T(8,128)(2,1)S(1)}, u32[]{:S(2)}, u32[]{:S(2)}) collective-permute-start(bf16[512,512]{1,0:T(8,128)(2,1)S(1)} %get-tuple-element.10), channel_id=1, source_target_pairs={{0,4},{1,5},{2,6},{3,7},{4,0},{5,1},{6,2},{7,3},{8,12},{9,13},{10,... | collective-permute-start | bytes 1572872 | tf_op jit(solution)/shard_map/ppermute | solution.py:17
  297.3 23.1 %collective-permute-start.16 = (bf16[512,512]{1,0:T(8,128)(2,1)S(1)}, bf16[512,512]{1,0:T(8,128)(2,1)S(1)}, u32[]{:S(2)}, u32[]{:S(2)}) collective-permute-start(bf16[512,512]{1,0:T(8,128)(2,1)S(1)} %get-tuple-element.9), channel_id=1, source_target_pairs={{0,6},{1,7},{2,0},{3,1},{4,2},{5,3},{6,4},{7,5},{8,14},{9,15},{10,... | collective-permute-start | bytes 1572872 | tf_op jit(solution)/shard_map/ppermute | solution.py:17
  328.0 11.4 %collective-permute-start.17 = (bf16[512,256]{1,0:T(8,128)(2,1)S(1)}, bf16[512,256]{1,0:T(8,128)(2,1)S(1)}, u32[]{:S(2)}, u32[]{:S(2)}) collective-permute-start(bf16[512,256]{1,0:T(8,128)(2,1)S(1)} %fusion.18), channel_id=1, source_target_pairs={{0,1},{1,0},{2,3},{3,2},{4,5},{5,4},{6,7},{7,6},{8,9},{9,8},{10,11... | collective-permute-start | bytes 786440 | tf_op jit(solution)/shard_map/ppermute | solution.py:21
  (1 other events, 1.3 us)
Sparse Core Ops, SparseCore 0:
  9.9 70.5 all-gather.1

commit v3 on v2

--- a/solution.py
+++ b/solution.py
@@ -1,11 +1,12 @@
 import jax
 import jax.numpy as jnp
 from jax import lax
-from jax.sharding import PartitionSpec as P
+from jax.sharding import Mesh, PartitionSpec as P
 from jax.experimental import pallas as pl
 from jax.experimental.pallas import tpu as pltpu
 
 HD = 64
+GRP = ("chips", "core")
 
 
 EPSILON = 1e-05
@@ -21,42 +22,56 @@
     return lax.ppermute(array, axis, [(i, i ^ 1 << bit) for i in range(lax.axis_size(axis))])
 
 
+def x_gather(pair):
+    rows, span = pair.shape
+    n_x = lax.axis_size("tp") // 2
+    mine_x = lax.axis_index("tp") // 2
+    full = jnp.zeros((rows, n_x * span), pair.dtype)
+    full = lax.dynamic_update_slice(full, pair, (0, mine_x * span))
+    for k in range(1, n_x):
+        got = shifted(pair, "tp", 2 * k)
+        full = lax.dynamic_update_slice(full, got, (0, ((mine_x - k) % n_x) * span))
+    return full
+
+
 def tp_gather(part):
-    rows, width = part.shape
-    n_x = lax.axis_size("tp") // 2
     me = lax.axis_index("tp")
-    mine_x = me // 2
     partner = swapped(part, "tp", 0)
-    low_first = me % 2 == 0
     pair = jnp.where(
-        low_first,
+        me % 2 == 0,
         jnp.concatenate([part, partner], axis=1),
         jnp.concatenate([partner, part], axis=1),
     )
-    full = jnp.zeros((rows, n_x * 2 * width), part.dtype)
-    full = lax.dynamic_update_slice(full, pair, (0, mine_x * 2 * width))
-    for k in range(1, n_x):
-        got = shifted(pair, "tp", 2 * k)
-        full = lax.dynamic_update_slice(full, got, (0, ((mine_x - k) % n_x) * 2 * width))
-    return full
-
-
-def tp_reduce(full):
+    return x_gather(pair)
+
+
+def x_reduce(full):
     rows, total_width = full.shape
     n_x = lax.axis_size("tp") // 2
-    me = lax.axis_index("tp")
-    mine_x = me // 2
+    mine_x = lax.axis_index("tp") // 2
     span = total_width // n_x
     acc = lax.dynamic_slice_in_dim(full, mine_x * span, span, 1).astype(jnp.float32)
     for k in range(1, n_x):
         piece = lax.dynamic_slice_in_dim(full, ((mine_x + k) % n_x) * span, span, 1)
         acc = acc + shifted(piece, "tp", 2 * k).astype(jnp.float32)
-    halves = acc.reshape(rows, 2, total_width // n_x // 2)
+    return acc
+
+
+def tp_reduce(full):
+    me = lax.axis_index("tp")
+    acc = x_reduce(full)
+    rows, span = acc.shape
+    halves = acc.reshape(rows, 2, span // 2)
     low = me % 2 == 0
     mine = jnp.where(low, halves[:, 0], halves[:, 1])
     other = jnp.where(low, halves[:, 1], halves[:, 0])
     got = swapped(other.astype(jnp.bfloat16), "tp", 0)
     return mine + got.astype(jnp.float32)
+
+
+def pair_reduce(full):
+    rounded = x_reduce(full).astype(jnp.bfloat16)
+    return rounded.astype(jnp.float32) + swapped(rounded, "tp", 0).astype(jnp.float32)
 
 
 def rms_normed(values, gain):
@@ -160,7 +175,7 @@
     query_local = w_query.shape[1] // HD
     stored_local = w_key.shape[1] // HD
     per_stored = query_local // stored_local
-    group_index = lax.axis_index("grp")
+    group_index = lax.axis_index(GRP)
     own_count = cache_len[group_index] - spill[group_index]
     far_count = spill[group_index]
     positions = cache_len[group_index] + jnp.arange(block, dtype=jnp.int32)
@@ -170,12 +185,23 @@
     store_values = cache_values.reshape(slots, stored_local, HD)
     second_ids = jnp.where(accept == 1, sub_ids, tok_ids)
 
-    table = lax.all_gather(embed, "grp", axis=0, tiled=True)
+    local_vocab = embed.shape[0]
+    core = lax.axis_index("core")
+    half = lax.all_gather(embed, "chips", axis=0, tiled=True)
+    other_half = lax.ppermute(half, "core", [(0, 1), (1, 0)])
     both_ids = jnp.concatenate([tok_ids, second_ids])
-    x_part = jnp.take(table, both_ids, axis=0)
+    owner = both_ids // local_vocab
+    at = (owner // 2) * local_vocab + both_ids % local_vocab
+    x_part = jnp.where(
+        (owner % 2 == core)[:, None],
+        jnp.take(half, at, axis=0),
+        jnp.take(other_half, at, axis=0),
+    )
     rows, width = x_part.shape
 
-    tail_keys, tail_values = swapped((cache_keys[block:], cache_values[block:]), "grp", 0)
+    tail_keys, tail_values = lax.ppermute(
+        (cache_keys[block:], cache_values[block:]), "core", [(0, 1), (1, 0)]
+    )
     far_keys = tail_keys.reshape(slots - block, stored_local, HD)
     far_values = tail_values.reshape(slots - block, stored_local, HD)
     far_valid = tail_ids >= slots - far_count
@@ -215,9 +241,13 @@
     )
     mixed = mixed_heads.reshape(rows, query_local * HD)
     head_term = jnp.dot(mixed, w_out, preferred_element_type=jnp.float32)
-    head_sum = tp_reduce(head_term.astype(jnp.bfloat16))
-    resid_part = (x_part.astype(jnp.float32) + head_sum).astype(jnp.bfloat16)
-    resid_full = tp_gather(resid_part)
+    head_pair = pair_reduce(head_term.astype(jnp.bfloat16))
+    span = head_pair.shape[1]
+    mine_x = lax.axis_index("tp") // 2
+    x_pair = lax.dynamic_slice_in_dim(x_full, mine_x * span, span, 1)
+    resid_pair = (x_pair.astype(jnp.float32) + head_pair).astype(jnp.bfloat16)
+    resid_full = x_gather(resid_pair)
+    resid_part = lax.dynamic_slice_in_dim(resid_pair, (lax.axis_index("tp") % 2) * width, width, 1)
     normed_mlp = rms_normed(resid_full.astype(jnp.float32), mlp_gain)
     gate = jnp.dot(normed_mlp, w_gate, preferred_element_type=jnp.float32)
     lift = jnp.dot(normed_mlp, w_up, preferred_element_type=jnp.float32)
@@ -229,13 +259,15 @@
 
 
 def solution(mesh):
+    n_grp, n_tp = mesh.shape["grp"], mesh.shape["tp"]
+    mesh = Mesh(mesh.devices.reshape(n_grp // 2, 2, n_tp), ("chips", "core", "tp"))
     placed = (
-        P("grp"),
-        P("grp"),
-        P("grp"),
-        P(),
-        P(),
-        P("grp", "tp"),
+        P(GRP),
+        P(GRP),
+        P(GRP),
+        P(),
+        P(),
+        P(GRP, "tp"),
         P(),
         P(None, "tp"),
         P(None, "tp"),
@@ -245,13 +277,13 @@
         P(None, "tp"),
         P(None, "tp"),
         P("tp", None),
-        P("grp", "tp"),
-        P("grp", "tp"),
+        P(GRP, "tp"),
+        P(GRP, "tp"),
     )
     return jax.shard_map(
         on_device,
         mesh=mesh,
         in_specs=placed,
-        out_specs=(P("grp", "tp"), P("grp", "tp")),
+        out_specs=(P(GRP, "tp"), P(GRP, "tp")),
         check_vma=False,
     )

time: 350 us -> 392 us (1.12)
  the two profiles are of different devices: /device:TPU:72 before, /device:TPU:14 now
where the time goes in v3:
time: 392 us; the launch traced here: 390 us
  waiting for transfers between devices  242 us (62%)
  local copies, waits for them, and re-layouts  48.8 us (12%)
  starting transfers between devices  22.1 us (6%)
  other arithmetic  21.1 us (5%)
  Pallas kernels  20.6 us (5%)
  matrix products  19 us (5%)
  between operations  16.5 us (4%)
    all_gather x1, waiting for transfers between devices, on_device(): half = lax.all_gather(embed, 'chips', axis=0, tiled=True)  105 us
    ppermute x12, waiting for transfers between devices, shifted(): return lax.ppermute(array, axis, [(i, (i + step) % n) for i in range(n)])  90.4 us
    ppermute x3, waiting for transfers between devices, swapped(): lax.ppermute(array, axis, [(i, i ^ 1 << bit) for i in range(lax.axis_size...  46.5 us
    pallas_call x1, Pallas kernels, attention(): pl.pallas_call(attention_kernel, grid=(passes, rows // tile), in_specs=[p...  20.6 us
    unnamed x38, local copies, waits for them, and re-layouts  13.3 us
    ppermute x12, starting transfers between devices, shifted(): return lax.ppermute(array, axis, [(i, (i + step) % n) for i in range(n)])  11.4 us
    ppermute x3, starting transfers between devices, swapped(): lax.ppermute(array, axis, [(i, i ^ 1 << bit) for i in range(lax.axis_size...  10.1 us
  transfers between devices with their start and end apart: 19, of which 16 were waited for; matrix products, arithmetic and copies ran while one was open for 14% of the time, Pallas kernels for 0%

profile of v3, /device:TPU:14, one launch (start us, length us, event | category | flops | bytes accessed | tf_op | source)
XLA Modules:
  0.0 390.3 jit_solution(12928381170839348278)
XLA Ops:
  8.0 104.5 %all-gather.2.cloned.1.call-done = bf16[8192,256]{1,0:T(8,128)(2,1)} async-done(((bf16[512,256]{1,0:T(8,128)(2,1)}), bf16[8192,256]{1,0:T(8,128)(2,1)}) %all-gather.2.cloned.1.call-update) | async-done | bytes 4194320 | tf_op jit(solution)/shard_map/all_gather | solution.py:190
  120.3 4.9 %gather_fusion = bf16[512,256]{1,0:T(8,128)(2,1)} fusion(bf16[8192,256]{1,0:T(8,128)(2,1)} %all-gather.2.cloned.1.call-done, s32[1024]{0:T(1024)S(1)} %pad_clamp_fusion), kind=kCustom, calls=%fused_computation.clone | custom fusion | bytes 526336 | tf_op jit(solution)/shard_map/jit(_take)/gather | solution.py:197
  125.2 5.0 %gather_fusion.1 = bf16[512,256]{1,0:T(8,128)(2,1)} fusion(bf16[8192,256]{1,0:T(8,128)(2,1)} %collective-permute-done, s32[1024]{0:T(1024)S(1)} %pad_clamp_fusion), kind=kCustom, calls=%fused_computation.1.clone | custom fusion | bytes 526336 | tf_op jit(solution)/shard_map/jit(_take)/gather | solution.py:198
  131.3 3.7 collective-permute-start.1
  137.5 12.0 %collective-permute-done.1 = bf16[512,256]{1,0:T(8,128)(2,1)S(1)} collective-permute-done((bf16[512,256]{1,0:T(8,128)(2,1)S(1)}, bf16[512,256]{1,0:T(8,128)(2,1)S(1)}, u32[]{:S(2)}, u32[]{:S(2)}) %collective-permute-start.1) | collective-permute-done | bytes 262176 | tf_op jit(solution)/shard_map/ppermute | solution.py:22
  153.4 2.5 collective-permute-start.3
  157.6 9.8 %collective-permute-done.2 = bf16[512,512]{1,0:T(8,128)(2,1)} collective-permute-done((bf16[512,512]{1,0:T(8,128)(2,1)}, bf16[512,512]{1,0:T(8,128)(2,1)}, u32[]{:S(2)}, u32[]{:S(2)}) %collective-permute-start.2) | collective-permute-done | bytes 524320 | tf_op jit(solution)/shard_map/ppermute | solution.py:18
  172.2 7.6 %collective-permute-done.4 = bf16[512,512]{1,0:T(8,128)(2,1)} collective-permute-done((bf16[512,512]{1,0:T(8,128)(2,1)}, bf16[512,512]{1,0:T(8,128)(2,1)}, u32[]{:S(2)}, u32[]{:S(2)}) %collective-permute-start.4) | collective-permute-done | bytes 524320 | tf_op jit(solution)/shard_map/ppermute | solution.py:18
  183.8 2.2 fusion.2
  191.5 2.6 fusion.34
  194.9 2.3 copy.40
  197.2 2.3 copy.41
  199.5 3.0 convolution_convert_fusion.2
  208.0 20.6 %shard_map.176 = bf16[2,1024,64]{2,1,0:T(8,128)(2,1)} custom-call(bf16[2,1024,64]{2,1,0:T(8,128)(2,1)} %pad_maximum_fusion.q_ref, bf16[2048,64]{1,0:T(8,128)(2,1)} %copy-done.3, bf16[1792,64]{1,0:T(8,128)(2,1)} %collective-permute-done.5.kf_ref, bf16[2,256,64]{2,1,0:T(8,128)(2,1)} %pad_maximum_fusion.1.kn_ref, bf16[2048,64]{1,0:T(8,128)(2,1)} %copy.36.vo_ref, ...), custom_call_target="tpu_custom_call" | custom-call | flops 2147483648 | bytes 1572864 | tf_op jit(solution)/shard_map/pallas_call | solution.py:130
  232.3 2.2 collective-permute-start.7
  235.5 11.6 %collective-permute-done.7 = bf16[512,512]{1,0:T(8,128)(2,1)S(1)} collective-permute-done((bf16[512,512]{1,0:T(8,128)(2,1)S(1)}, bf16[512,512]{1,0:T(8,128)(2,1)S(1)}, u32[]{:S(2)}, u32[]{:S(2)}) %collective-permute-start.7) | collective-permute-done | bytes 524320 | tf_op jit(solution)/shard_map/ppermute | solution.py:18
  247.1 3.7 collective-permute-done.8
  250.8 8.7 %collective-permute-done.9 = bf16[512,512]{1,0:T(8,128)(2,1)S(1)} collective-permute-done((bf16[512,512]{1,0:T(8,128)(2,1)S(1)}, bf16[512,512]{1,0:T(8,128)(2,1)S(1)}, u32[]{:S(2)}, u32[]{:S(2)}) %collective-permute-start.9) | collective-permute-done | bytes 524320 | tf_op jit(solution)/shard_map/ppermute | solution.py:18
  259.8 3.9 collective-permute-start.10
  263.7 24.6 %collective-permute-done.10 = bf16[512,512]{1,0:T(8,128)(2,1)S(1)} collective-permute-done((bf16[512,512]{1,0:T(8,128)(2,1)S(1)}, bf16[512,512]{1,0:T(8,128)(2,1)S(1)}, u32[]{:S(2)}, u32[]{:S(2)}) %collective-permute-start.10) | collective-permute-done | bytes 524320 | tf_op jit(solution)/shard_map/ppermute | solution.py:22
  292.4 12.3 %collective-permute-done.11 = bf16[512,512]{1,0:T(8,128)(2,1)S(1)} collective-permute-done((bf16[512,512]{1,0:T(8,128)(2,1)S(1)}, bf16[512,512]{1,0:T(8,128)(2,1)S(1)}, u32[]{:S(2)}, u32[]{:S(2)}) %collective-permute-start.11) | collective-permute-done | bytes 524320 | tf_op jit(solution)/shard_map/ppermute | solution.py:18
  306.6 10.1 %collective-permute-done.13 = bf16[512,512]{1,0:T(8,128)(2,1)S(1)} collective-permute-done((bf16[512,512]{1,0:T(8,128)(2,1)S(1)}, bf16[512,512]{1,0:T(8,128)(2,1)S(1)}, u32[]{:S(2)}, u32[]{:S(2)}) %collective-permute-start.13) | collective-permute-done | bytes 524320 | tf_op jit(solution)/shard_map/ppermute | solution.py:18
  318.0 2.9 fusion.11
  320.9 7.8 %convolution_convert_fusion.1 = bf16[512,2048]{1,0:T(8,128)(2,1)} fusion(bf16[704,2048]{1,0:T(8,128)(2,1)S(1)} %copy-done, f32[512,704]{0,1:T(8,128)} %fusion.11, bf16[2048,704]{0,1:T(8,128)(2,1)} %param.32, bf16[512,2048]{1,0:T(8,128)(2,1)} %copy-done.2, f32[2048]{0:T(1024)S(1)} %copy-done.13, f32[512]{0:T(512)S(1)} %add_rsqrt_fusion), kind=kOutput, calls=%fused_computation.13 | convolution fusion | flops 2960195584 | bytes 11413504 | tf_op jit(solution)/shard_map/dot_general | solution.py:255
  332.8 12.3 %collective-permute-done.14 = bf16[512,512]{1,0:T(8,128)(2,1)S(1)} collective-permute-done((bf16[512,512]{1,0:T(8,128)(2,1)S(1)}, bf16[512,512]{1,0:T(8,128)(2,1)S(1)}, u32[]{:S(2)}, u32[]{:S(2)}) %collective-permute-start.14) | collective-permute-done | bytes 524320 | tf_op jit(solution)/shard_map/ppermute | solution.py:18
  345.1 2.8 collective-permute-done.15
  347.8 9.1 %collective-permute-done.16 = bf16[512,512]{1,0:T(8,128)(2,1)S(1)} collective-permute-done((bf16[512,512]{1,0:T(8,128)(2,1)S(1)}, bf16[512,512]{1,0:T(8,128)(2,1)S(1)}, u32[]{:S(2)}, u32[]{:S(2)}) %collective-permute-start.16) | collective-permute-done | bytes 524320 | tf_op jit(solution)/shard_map/ppermute | solution.py:18
  357.0 2.3 convert_add_fusion
  359.3 2.6 copy.37
  361.8 2.2 fusion.31
  369.1 2.6 collective-permute-start.17
  371.7 9.9 %collective-permute-done.17 = bf16[512,256]{1,0:T(8,128)(2,1)} collective-permute-done((bf16[512,256]{1,0:T(8,128)(2,1)}, bf16[512,256]{1,0:T(8,128)(2,1)}, u32[]{:S(2)}, u32[]{:S(2)}) %collective-permute-start.17) | collective-permute-done | bytes 262176 | tf_op jit(solution)/shard_map/ppermute | solution.py:22
  (102 shorter events, 59.5 us)
Async XLA Ops:
  7.2 313.8 %copy-start = (bf16[704,2048]{1,0:T(8,128)(2,1)S(1)}, bf16[704,2048]{1,0:T(8,128)(2,1)}, u32[]{:S(2)}) copy-start(bf16[704,2048]{1,0:T(8,128)(2,1)} %param.33) | copy-start | bytes 8650756
  7.2 111.8 %copy-start.14 = (s32[32]{0:T(128)S(1)}, s32[32]{0:T(128)}, u32[]{:S(2)}) copy-start(s32[32]{0:T(128)} %param.23) | copy-start | bytes 388
  7.2 113.0 %copy-start.9 = (s32[256]{0:T(256)S(1)}, s32[256]{0:T(256)}, u32[]{:S(2)}) copy-start(s32[256]{0:T(256)} %param.19) | copy-start | bytes 3076
  7.2 113.0 %copy-start.11 = (s32[256]{0:T(256)S(1)}, s32[256]{0:T(256)}, u32[]{:S(2)}) copy-start(s32[256]{0:T(256)} %param.20) | copy-start | bytes 3076
  7.2 113.0 %copy-start.10 = (s32[256]{0:T(256)S(1)}, s32[256]{0:T(256)}, u32[]{:S(2)}) copy-start(s32[256]{0:T(256)} %param.21) | copy-start | bytes 3076
  7.2 105.3 %all-gather.2.cloned.1.call-start = ((), (), s32[]{:S(2)}) async-start(), calls=%async_computation | async-start | bytes 4456448 | tf_op jit(solution)/shard_map/all_gather | solution.py:190
  112.5 12.7 %collective-permute-start = (bf16[8192,256]{1,0:T(8,128)(2,1)}, bf16[8192,256]{1,0:T(8,128)(2,1)}, u32[]{:S(2)}, u32[]{:S(2)}) collective-permute-start(bf16[8192,256]{1,0:T(8,128)(2,1)} %all-gather.2.cloned.1.call-done), channel_id=1, source_target_pairs={{0,8},{8,0},{1,9},{9,1},{2,10},{10,2},{3,11},{11,3},{4,12},{12,4},... | collective-permute-start | bytes 12582920 | tf_op jit(solution)/shard_map/ppermute | solution.py:191
  113.7 11.5 %copy-start.3 = (bf16[2048,64]{1,0:T(8,128)(2,1)}, bf16[2048,64]{1,0:T(8,128)(2,1)S(1)}, u32[]{:S(2)}) copy-start(bf16[2048,64]{1,0:T(8,128)(2,1)S(1)} %copy.35.ko_ref) | copy-start | bytes 786436
  114.6 93.4 %collective-permute-start.5 = (bf16[1792,64]{1,0:T(8,128)(2,1)}, bf16[1792,64]{1,0:T(8,128)(2,1)}, u32[]{:S(2)}, u32[]{:S(2)}) collective-permute-start(bf16[1792,64]{1,0:T(8,128)(2,1)} %slice.52), channel_id=1, source_target_pairs={{0,8},{8,0},{1,9},{9,1},{2,10},{10,2},{3,11},{11,3},{4,12},{12,4},... | collective-permute-start | bytes 688136 | tf_op jit(solution)/shard_map/ppermute | solution.py:202
  118.9 89.1 %collective-permute-start.6 = (bf16[1792,64]{1,0:T(8,128)(2,1)}, bf16[1792,64]{1,0:T(8,128)(2,1)}, u32[]{:S(2)}, u32[]{:S(2)}) collective-permute-start(bf16[1792,64]{1,0:T(8,128)(2,1)} %slice.55), channel_id=1, source_target_pairs={{0,8},{8,0},{1,9},{9,1},{2,10},{10,2},{3,11},{11,3},{4,12},{12,4},... | collective-permute-start | bytes 688136 | tf_op jit(solution)/shard_map/ppermute | solution.py:202
  125.2 9.8 %copy-start.15 = (s32[32]{0:T(128)S(1)}, s32[32]{0:T(128)}, u32[]{:S(2)}) copy-start(s32[32]{0:T(128)} %param.22) | copy-start | bytes 388
  125.2 5.0 %copy-start.5 = (bf16[512,256]{1,0:T(8,128)(2,1)S(1)}, bf16[512,256]{1,0:T(8,128)(2,1)}, u32[]{:S(2)}) copy-start(bf16[512,256]{1,0:T(8,128)(2,1)} %gather_fusion) | copy-start | bytes 786436
  131.3 18.2 %collective-permute-start.1 = (bf16[512,256]{1,0:T(8,128)(2,1)S(1)}, bf16[512,256]{1,0:T(8,128)(2,1)S(1)}, u32[]{:S(2)}, u32[]{:S(2)}) collective-permute-start(bf16[512,256]{1,0:T(8,128)(2,1)S(1)} %select_select_fusion), channel_id=1, source_target_pairs={{0,1},{1,0},{2,3},{3,2},{4,5},{5,4},{6,7},{7,6},{8,9},{9,8},{10,11... | collective-permute-start | bytes 786440 | tf_op jit(solution)/shard_map/ppermute | solution.py:22
  152.3 15.2 %collective-permute-start.2 = (bf16[512,512]{1,0:T(8,128)(2,1)}, bf16[512,512]{1,0:T(8,128)(2,1)}, u32[]{:S(2)}, u32[]{:S(2)}) collective-permute-start(bf16[512,512]{1,0:T(8,128)(2,1)} %get-tuple-element.6), channel_id=1, source_target_pairs={{0,2},{1,3},{2,4},{3,5},{4,6},{5,7},{6,0},{7,1},{8,10},{9,11},{10,... | collective-permute-start | bytes 1572872 | tf_op jit(solution)/shard_map/ppermute | solution.py:18
  153.4 16.8 %collective-permute-start.3 = (bf16[512,512]{1,0:T(8,128)(2,1)}, bf16[512,512]{1,0:T(8,128)(2,1)}, u32[]{:S(2)}, u32[]{:S(2)}) collective-permute-start(bf16[512,512]{1,0:T(8,128)(2,1)} %get-tuple-element.6), channel_id=1, source_target_pairs={{0,4},{1,5},{2,6},{3,7},{4,0},{5,1},{6,2},{7,3},{8,12},{9,13},{10,... | collective-permute-start | bytes 1572872 | tf_op jit(solution)/shard_map/ppermute | solution.py:18
  155.9 23.9 %collective-permute-start.4 = (bf16[512,512]{1,0:T(8,128)(2,1)}, bf16[512,512]{1,0:T(8,128)(2,1)}, u32[]{:S(2)}, u32[]{:S(2)}) collective-permute-start(bf16[512,512]{1,0:T(8,128)(2,1)} %get-tuple-element.6), channel_id=1, source_target_pairs={{0,6},{1,7},{2,0},{3,1},{4,2},{5,3},{6,4},{7,5},{8,14},{9,15},{10,... | collective-permute-start | bytes 1572872 | tf_op jit(solution)/shard_map/ppermute | solution.py:18
  169.3 14.4 %copy-start.8 = (f32[2048]{0:T(1024)S(1)}, f32[2048]{0:T(1024)}, u32[]{:S(2)}) copy-start(f32[2048]{0:T(1024)} %param.25) | copy-start | bytes 24580
  183.8 3.6 copy-start.7
  232.3 14.9 %collective-permute-start.7 = (bf16[512,512]{1,0:T(8,128)(2,1)S(1)}, bf16[512,512]{1,0:T(8,128)(2,1)S(1)}, u32[]{:S(2)}, u32[]{:S(2)}) collective-permute-start(bf16[512,512]{1,0:T(8,128)(2,1)S(1)} %get-tuple-element.14), channel_id=1, source_target_pairs={{0,2},{1,3},{2,4},{3,5},{4,6},{5,7},{6,0},{7,1},{8,10},{9,11},{10,... | collective-permute-start | bytes 1572872 | tf_op jit(solution)/shard_map/ppermute | solution.py:18
  234.4 16.4 %collective-permute-start.8 = (bf16[512,512]{1,0:T(8,128)(2,1)S(1)}, bf16[512,512]{1,0:T(8,128)(2,1)S(1)}, u32[]{:S(2)}, u32[]{:S(2)}) collective-permute-start(bf16[512,512]{1,0:T(8,128)(2,1)S(1)} %get-tuple-element.16), channel_id=1, source_target_pairs={{0,4},{1,5},{2,6},{3,7},{4,0},{5,1},{6,2},{7,3},{8,12},{9,13},{10,... | collective-permute-start | bytes 1572872 | tf_op jit(solution)/shard_map/ppermute | solution.py:18
  235.3 24.1 %collective-permute-start.9 = (bf16[512,512]{1,0:T(8,128)(2,1)S(1)}, bf16[512,512]{1,0:T(8,128)(2,1)S(1)}, u32[]{:S(2)}, u32[]{:S(2)}) collective-permute-start(bf16[512,512]{1,0:T(8,128)(2,1)S(1)} %get-tuple-element.15), channel_id=1, source_target_pairs={{0,6},{1,7},{2,0},{3,1},{4,2},{5,3},{6,4},{7,5},{8,14},{9,15},{10,... | collective-permute-start | bytes 1572872 | tf_op jit(solution)/shard_map/ppermute | solution.py:18
  259.8 28.5 %collective-permute-start.10 = (bf16[512,512]{1,0:T(8,128)(2,1)S(1)}, bf16[512,512]{1,0:T(8,128)(2,1)S(1)}, u32[]{:S(2)}, u32[]{:S(2)}) collective-permute-start(bf16[512,512]{1,0:T(8,128)(2,1)S(1)} %add_convert_fusion.1), channel_id=1, source_target_pairs={{0,1},{1,0},{2,3},{3,2},{4,5},{5,4},{6,7},{7,6},{8,9},{9,8},{10,11... | collective-permute-start | bytes 1572872 | tf_op jit(solution)/shard_map/ppermute | solution.py:22
  289.8 27.3 %copy-start.4 = (bf16[512,512]{1,0:T(8,128)(2,1)}, bf16[512,512]{1,0:T(8,128)(2,1)S(1)}, u32[]{:S(2)}) copy-start(bf16[512,512]{1,0:T(8,128)(2,1)S(1)} %get-tuple-element.4) | copy-start | bytes 1572868
  289.9 14.9 %collective-permute-start.11 = (bf16[512,512]{1,0:T(8,128)(2,1)S(1)}, bf16[512,512]{1,0:T(8,128)(2,1)S(1)}, u32[]{:S(2)}, u32[]{:S(2)}) collective-permute-start(bf16[512,512]{1,0:T(8,128)(2,1)S(1)} %get-tuple-element.4), channel_id=1, source_target_pairs={{0,2},{1,3},{2,4},{3,5},{4,6},{5,7},{6,0},{7,1},{8,10},{9,11},{10,... | collective-permute-start | bytes 1572872 | tf_op jit(solution)/shard_map/ppermute | solution.py:18
  290.2 16.4 %collective-permute-start.12 = (bf16[512,512]{1,0:T(8,128)(2,1)S(1)}, bf16[512,512]{1,0:T(8,128)(2,1)S(1)}, u32[]{:S(2)}, u32[]{:S(2)}) collective-permute-start(bf16[512,512]{1,0:T(8,128)(2,1)S(1)} %get-tuple-element.4), channel_id=1, source_target_pairs={{0,4},{1,5},{2,6},{3,7},{4,0},{5,1},{6,2},{7,3},{8,12},{9,13},{10,... | collective-permute-start | bytes 1572872 | tf_op jit(solution)/shard_map/ppermute | solution.py:18
  291.1 25.5 %collective-permute-start.13 = (bf16[512,512]{1,0:T(8,128)(2,1)S(1)}, bf16[512,512]{1,0:T(8,128)(2,1)S(1)}, u32[]{:S(2)}, u32[]{:S(2)}) collective-permute-start(bf16[512,512]{1,0:T(8,128)(2,1)S(1)} %get-tuple-element.4), channel_id=1, source_target_pairs={{0,6},{1,7},{2,0},{3,1},{4,2},{5,3},{6,4},{7,5},{8,14},{9,15},{10,... | collective-permute-start | bytes 1572872 | tf_op jit(solution)/shard_map/ppermute | solution.py:18
  304.8 13.2 %copy-start.12 = (bf16[2048,704]{0,1:T(8,128)(2,1)S(1)}, bf16[2048,704]{0,1:T(8,128)(2,1)}, u32[]{:S(2)}) copy-start(bf16[2048,704]{0,1:T(8,128)(2,1)} %param.31) | copy-start | bytes 8650756
  304.8 13.2 %copy-start.13 = (f32[2048]{0:T(1024)S(1)}, f32[2048]{0:T(1024)}, u32[]{:S(2)}) copy-start(f32[2048]{0:T(1024)} %param.30) | copy-start | bytes 24580
  330.2 14.9 %collective-permute-start.14 = (bf16[512,512]{1,0:T(8,128)(2,1)S(1)}, bf16[512,512]{1,0:T(8,128)(2,1)S(1)}, u32[]{:S(2)}, u32[]{:S(2)}) collective-permute-start(bf16[512,512]{1,0:T(8,128)(2,1)S(1)} %get-tuple-element.11), channel_id=1, source_target_pairs={{0,2},{1,3},{2,4},{3,5},{4,6},{5,7},{6,0},{7,1},{8,10},{9,11},{10,... | collective-permute-start | bytes 1572872 | tf_op jit(solution)/shard_map/ppermute | solution.py:18
  331.4 16.4 %collective-permute-start.15 = (bf16[512,512]{1,0:T(8,128)(2,1)S(1)}, bf16[512,512]{1,0:T(8,128)(2,1)S(1)}, u32[]{:S(2)}, u32[]{:S(2)}) collective-permute-start(bf16[512,512]{1,0:T(8,128)(2,1)S(1)} %get-tuple-element.13), channel_id=1, source_target_pairs={{0,4},{1,5},{2,6},{3,7},{4,0},{5,1},{6,2},{7,3},{8,12},{9,13},{10,... | collective-permute-start | bytes 1572872 | tf_op jit(solution)/shard_map/ppermute | solution.py:18
  332.0 25.0 %collective-permute-start.16 = (bf16[512,512]{1,0:T(8,128)(2,1)S(1)}, bf16[512,512]{1,0:T(8,128)(2,1)S(1)}, u32[]{:S(2)}, u32[]{:S(2)}) collective-permute-start(bf16[512,512]{1,0:T(8,128)(2,1)S(1)} %get-tuple-element.12), channel_id=1, source_target_pairs={{0,6},{1,7},{2,0},{3,1},{4,2},{5,3},{6,4},{7,5},{8,14},{9,15},{10,... | collective-permute-start | bytes 1572872 | tf_op jit(solution)/shard_map/ppermute | solution.py:18
  369.1 12.5 %collective-permute-start.17 = (bf16[512,256]{1,0:T(8,128)(2,1)}, bf16[512,256]{1,0:T(8,128)(2,1)}, u32[]{:S(2)}, u32[]{:S(2)}) collective-permute-start(bf16[512,256]{1,0:T(8,128)(2,1)} %fusion.15), channel_id=1, source_target_pairs={{0,1},{1,0},{2,3},{3,2},{4,5},{5,4},{6,7},{7,6},{8,9},{9,8},{10,11... | collective-permute-start | bytes 786440 | tf_op jit(solution)/shard_map/ppermute | solution.py:22
  (3 other events, 4.8 us)
Sparse Core Ops, SparseCore 0:
  9.8 102.6 all-gather.1
